TPU v7x, 256 devices: a whole 4x4x8 slice. The times are simulated.
256 devices in a mesh: segment: 2 (over y_lo), gx: 8 (over x, y_hi), gy: 16 (over z, core).
Axes of the slice: x: 4, y: 4 (y_hi: 2, y_lo: 2; y = y_hi * 2 + y_lo), z: 8, core: 2. Of those that a mesh axis runs over, the one named last changes fastest.
Arguments:
- node_latent: bfloat16 [131072, 512], P(('segment', 'gx', 'gy')), may hold values from -6 to 6
- edge_latent: bfloat16 [262144, 512], P(('segment', 'gx', 'gy')), may hold values from -6 to 6
- adjacency: bfloat16 [1024, 2, 128, 128], P(('segment', 'gx', 'gy')), may hold values from -0.5 to 0.5
- neighbours: int32 [1024, 2], P(('segment', 'gx', 'gy')), may hold values from 0 to 9, as said below
- live: int32 [1024, 2], P(('segment', 'gx', 'gy')), may hold values 0 or 1
- send_blocks: int32 [256, 6], P(('segment', 'gx', 'gy')), may hold values from 0 to 3
- w_edge_in: bfloat16 [1536, 512], replicated, may hold values from -0.15625 to 0.15625
- w_edge_out: bfloat16 [512, 512], replicated, may hold values from -0.25 to 0.25
- w_node_in: bfloat16 [1024, 512], replicated, may hold values from -0.1875 to 0.1875
- w_node_out: bfloat16 [512, 512], replicated, may hold values from -0.25 to 0.25
- node_cotangent: bfloat16 [131072, 512], P(('segment', 'gx', 'gy')), may hold values from -6 to 6
- edge_cotangent: bfloat16 [262144, 512], P(('segment', 'gx', 'gy')), may hold values from -6 to 6
Outputs:
- node_out: bfloat16 [131072, 512], P(('segment', 'gx', 'gy'))
- edge_out: bfloat16 [262144, 512], P(('segment', 'gx', 'gy'))
- node_grad: float32 [131072, 512], P(('segment', 'gx', 'gy'))
- grad_edge_in: float32 [786432], P(('segment', 'gx', 'gy'))
- grad_edge_out: float32 [262144], P(('segment', 'gx', 'gy'))
- grad_node_in: float32 [524288], P(('segment', 'gx', 'gy'))
- grad_node_out: float32 [262144], P(('segment', 'gx', 'gy'))
Inputs may be any that keep to these rules, and one draw needn't show every extreme that they name: `neighbours`: indices below 4 name the device's own blocks, 4 + j names received block j; on every device each of the six received blocks is named by at least one slot.
All inputs are finite; a program needn't handle non-finite values. No bound on the sum of `live` on one device may be relied on, other than what follows from the above.
Results may differ from a plain program's by a relative error of at most 0.014.
Values may be sent and summed in bfloat16 or wider, within the bound.
No kernel may reach another device: no remote copies, remote signals or barrier semaphores. Data moves between devices by JAX's collectives and lax.ppermute only.
A program may use at most 128 MiB of HBM per device.

v0:
```python
from functools import partial

import jax
import jax.numpy as jnp
from jax import lax
from jax.sharding import PartitionSpec as P


def passed_along(block, axis, distance):
    devices = range(lax.axis_size(axis))
    route = [(i - distance, i) for i in devices if i - distance in devices]
    return lax.ppermute(block, axis, route)


def layer_norm(values):
    average = jnp.mean(values, axis=-1, keepdims=True)
    centred = values - average
    return centred * lax.rsqrt(jnp.mean(centred * centred, axis=-1, keepdims=True) + 1e-05)


def edge_part(node_blocks, received, w_edge_in, w_edge_out, edge_rows, adjacency_tiles, picker):
    latent = node_blocks.shape[-1]
    blocks = node_blocks.shape[0]
    block_rows = node_blocks.shape[1]
    degree = picker.shape[0] // blocks
    extended = jnp.concatenate([node_blocks, received], axis=0)
    sources = jnp.einsum(
        "sn,nbd->sbd", picker, extended, preferred_element_type=jnp.float32
    ).astype(jnp.bfloat16)
    mixed_rows = jnp.einsum(
        "sij,sjd->sid", adjacency_tiles, sources, preferred_element_type=jnp.float32
    ).astype(jnp.bfloat16)
    self_term = jnp.dot(
        node_blocks.reshape(-1, latent),
        w_edge_in[latent : 2 * latent],
        preferred_element_type=jnp.float32,
    )
    pre_edge = jnp.dot(edge_rows, w_edge_in[:latent], preferred_element_type=jnp.float32) + jnp.dot(
        mixed_rows.reshape(-1, latent), w_edge_in[2 * latent :], preferred_element_type=jnp.float32
    )
    pre_edge = (
        pre_edge.reshape(blocks, degree, block_rows, latent)
        + self_term.reshape(blocks, 1, block_rows, latent)
    ).reshape(-1, latent)
    edge_hidden = jax.nn.silu(pre_edge).astype(jnp.bfloat16)
    return layer_norm(jnp.dot(edge_hidden, w_edge_out, preferred_element_type=jnp.float32))


def node_part(node_blocks, messages, w_node_in, w_node_out, edge_rows, live_weight):
    latent = node_blocks.shape[-1]
    blocks = node_blocks.shape[0]
    block_rows = node_blocks.shape[1]
    edges_out = (edge_rows.astype(jnp.float32) + messages).astype(jnp.bfloat16)
    gathered = jnp.sum(
        messages.reshape(blocks, -1, block_rows, latent) * live_weight[:, :, None, None], axis=1
    ).astype(jnp.bfloat16)
    flat_nodes = node_blocks.reshape(-1, latent)
    pre_node = jnp.dot(
        flat_nodes, w_node_in[:latent], preferred_element_type=jnp.float32
    ) + jnp.dot(
        gathered.reshape(-1, latent), w_node_in[latent:], preferred_element_type=jnp.float32
    )
    node_hidden = jax.nn.silu(pre_node).astype(jnp.bfloat16)
    nodes_out = (
        flat_nodes.astype(jnp.float32)
        + layer_norm(jnp.dot(node_hidden, w_node_out, preferred_element_type=jnp.float32))
    ).astype(jnp.bfloat16)
    return (nodes_out, edges_out)


def across_rows(face_rows, offset):
    return passed_along(face_rows, "gx", offset)


def across_cols(face_rows, offset):
    return passed_along(face_rows, "gy", offset)


def across_segment(face_rows, offset):
    return passed_along(face_rows, "segment", offset)


def swap_faces(face_blocks):
    return jnp.stack(
        [
            across_rows(face_blocks[1], 1),
            across_rows(face_blocks[0], -1),
            across_cols(face_blocks[3], 1),
            across_cols(face_blocks[2], -1),
            across_segment(face_blocks[5], 1),
            across_segment(face_blocks[4], -1),
        ],
        axis=0,
    )


def shards(
    node_latent,
    edge_latent,
    adjacency,
    neighbours,
    live,
    send_blocks,
    w_edge_in,
    w_edge_out,
    w_node_in,
    w_node_out,
    node_cotangent,
    edge_cotangent,
):
    latent = node_latent.shape[1]
    blocks, degree = neighbours.shape
    block_rows = adjacency.shape[-1]
    node_blocks = node_latent.reshape(blocks, block_rows, latent)
    choose = (send_blocks[0][:, None] == jnp.arange(blocks, dtype=jnp.int32)[None, :]).astype(
        jnp.bfloat16
    )
    outgoing = jnp.einsum(
        "jn,nbd->jbd", choose, node_blocks, preferred_element_type=jnp.float32
    ).astype(jnp.bfloat16)
    received = swap_faces(outgoing)
    adjacency_tiles = adjacency.reshape(blocks * degree, block_rows, block_rows)
    picker = (
        neighbours.reshape(-1)[:, None] == jnp.arange(blocks + 6, dtype=jnp.int32)[None, :]
    ).astype(jnp.bfloat16)
    live_weight = live.astype(jnp.float32)
    messages, edge_pull = jax.vjp(
        partial(edge_part, edge_rows=edge_latent, adjacency_tiles=adjacency_tiles, picker=picker),
        node_blocks,
        received,
        w_edge_in,
        w_edge_out,
    )
    outputs, node_pull = jax.vjp(
        partial(node_part, edge_rows=edge_latent, live_weight=live_weight),
        node_blocks,
        messages,
        w_node_in,
        w_node_out,
    )
    node_direct, message_ct, grad_ni, grad_no = node_pull((node_cotangent, edge_cotangent))
    node_terms = (grad_ni.astype(jnp.float32).reshape(-1), grad_no.astype(jnp.float32).reshape(-1))
    node_indirect, received_ct, grad_ei, grad_eo = edge_pull(message_ct)
    returned = swap_faces(received_ct)
    node_grad = node_direct.astype(jnp.float32) + node_indirect.astype(jnp.float32)
    node_grad = node_grad + jnp.einsum(
        "jn,jbd->nbd", choose, returned, preferred_element_type=jnp.float32
    )
    edge_terms = (grad_ei.astype(jnp.float32).reshape(-1), grad_eo.astype(jnp.float32).reshape(-1))
    shares = (
        lax.psum_scatter(edge_terms[0], ("segment", "gx", "gy"), scatter_dimension=0, tiled=True),
        lax.psum_scatter(edge_terms[1], ("segment", "gx", "gy"), scatter_dimension=0, tiled=True),
        lax.psum_scatter(node_terms[0], ("segment", "gx", "gy"), scatter_dimension=0, tiled=True),
        lax.psum_scatter(node_terms[1], ("segment", "gx", "gy"), scatter_dimension=0, tiled=True),
    )
    return (
        outputs[0],
        outputs[1],
        node_grad.reshape(-1, latent),
        shares[0],
        shares[1],
        shares[2],
        shares[3],
    )


def solution(mesh):
    placed = (
        P(("segment", "gx", "gy"), None),
        P(("segment", "gx", "gy"), None),
        P(("segment", "gx", "gy"), None, None, None),
        P(("segment", "gx", "gy"), None),
        P(("segment", "gx", "gy"), None),
        P(("segment", "gx", "gy"), None),
        P(),
        P(),
        P(),
        P(),
        P(("segment", "gx", "gy"), None),
        P(("segment", "gx", "gy"), None),
    )
    return jax.shard_map(
        shards,
        mesh=mesh,
        in_specs=placed,
        out_specs=(
            P(("segment", "gx", "gy"), None),
            P(("segment", "gx", "gy"), None),
            P(("segment", "gx", "gy"), None),
            P(("segment", "gx", "gy")),
            P(("segment", "gx", "gy")),
            P(("segment", "gx", "gy")),
            P(("segment", "gx", "gy")),
        ),
        check_vma=False,
    )
```

profile of v0, /device:TPU:16, one launch (start us, length us, event | category | flops | bytes accessed | tf_op | source)
XLA Modules:
  0.0 395.3 jit_solution(11438302464971292038)
XLA Ops:
  7.2 1.7 convolution_convert_fusion.4
  8.9 1.2 fusion.68
  10.1 3.2 collective-permute-start
  13.3 4.2 %collective-permute-start.1 = (bf16[128,512]{1,0:T(8,128)(2,1)S(1)}, bf16[128,512]{1,0:T(8,128)(2,1)S(1)}, u32[]{:S(2)}, u32[]{:S(2)}) collective-permute-start(bf16[128,512]{1,0:T(8,128)(2,1)S(1)} %bitcast.158), channel_id=1, source_target_pairs={{16,0},{32,16},{48,32},{64,48},{80,64},{96,80},{112,96},{17,1},{33... | collective-permute-start | bytes 393224 | tf_op jit(solution)/shard_map/ppermute | solution.py:12
  18.2 1.9 collective-permute-start.2
  20.8 1.4 collective-permute-start.3
  22.9 3.8 collective-permute-start.4
  26.7 2.0 fusion.38
  28.8 1.4 fusion.43
  30.8 1.5 collective-permute-start.5
  32.3 1.4 fusion.48
  33.7 1.2 copy.204
  35.2 1.3 copy.213
  36.7 0.9 copy.205
  37.6 0.9 copy.206
  38.5 1.8 copy.207
  40.3 1.8 copy.208
  42.1 1.8 copy.209
  43.9 1.8 copy.210
  45.7 10.9 %concatenate.3 = bf16[10,128,512]{2,0,1:T(8,128)(2,1)} concatenate(bf16[4,128,512]{2,0,1:T(4,128)(2,1)} %copy.204, bf16[1,128,512]{2,0,1:T(2,128)(2,1)} %copy.205, bf16[1,128,512]{2,0,1:T(2,128)(2,1)} %copy.206, bf16[1,128,512]{2,0,1:T(2,128)(2,1)} %copy.207, bf16[1,128,512]{2,0,1:T(2,128)(2,1)} %copy.208, bf16[1,128,512]{2,0,1:T(2,128)(2,1)} %copy.209, bf16[1,128,512]{2,0,1:T(2,128)(2,1)} %copy.210), dimensions={0} | concatenate | bytes 2621440 | tf_op jit(solution)/shard_map/jvp()/concatenate | solution.py:26
  56.6 2.2 convolution_convert_fusion.5
  59.7 1.8 bitcast_add_fusion
  62.8 1.4 add_convert_fusion
  67.1 1.2 fusion.62
  71.3 1.5 fusion.66
  72.9 1.3 fusion
  74.2 1.6 fusion.25
  75.8 1.6 fusion.71
  77.4 2.0 fusion.17
  79.3 1.3 fusion.24
  80.6 1.3 fusion.72
  81.9 1.8 fusion.21
  83.7 1.1 reduce_sum.115
  84.8 1.5 fusion.23
  86.4 1.5 convert_bitcast_fusion
  87.9 2.5 copy.246
  90.3 1.2 copy.247
  91.9 1.9 copy.248
  93.8 1.3 copy.249
  95.1 1.8 convolution_convert_fusion.1
  97.4 1.7 copy.216
  99.1 2.0 convolution_convert_fusion
  101.2 1.2 fusion.67
  102.4 4.5 %collective-permute-start.6 = (bf16[128,512]{1,0:T(8,128)(2,1)S(1)}, bf16[128,512]{1,0:T(8,128)(2,1)S(1)}, u32[]{:S(2)}, u32[]{:S(2)}) collective-permute-start(bf16[128,512]{1,0:T(8,128)(2,1)S(1)} %bitcast.164), channel_id=1, source_target_pairs={{0,16},{16,32},{32,48},{48,64},{64,80},{80,96},{96,112},{1,17},{17... | collective-permute-start | bytes 393224 | tf_op jit(solution)/shard_map/ppermute | solution.py:12
  107.5 3.1 collective-permute-start.7
  111.3 4.3 %collective-permute-start.8 = (bf16[128,512]{1,0:T(8,128)(2,1)}, bf16[128,512]{1,0:T(8,128)(2,1)}, u32[]{:S(2)}, u32[]{:S(2)}) collective-permute-start(bf16[128,512]{1,0:T(8,128)(2,1)} %bitcast.127), channel_id=1, source_target_pairs={{0,1},{1,2},{2,3},{3,4},{4,5},{5,6},{6,7},{7,8},{8,9},{9,10},{10,1... | collective-permute-start | bytes 393224 | tf_op jit(solution)/shard_map/ppermute | solution.py:12
  116.3 1.3 collective-permute-start.9
  118.3 5.4 %collective-permute-start.10 = (bf16[128,512]{1,0:T(8,128)(2,1)}, bf16[128,512]{1,0:T(8,128)(2,1)}, u32[]{:S(2)}, u32[]{:S(2)}) collective-permute-start(bf16[128,512]{1,0:T(8,128)(2,1)} %bitcast.125), channel_id=1, source_target_pairs={{0,128},{1,129},{2,130},{3,131},{4,132},{5,133},{6,134},{7,135},{8... | collective-permute-start | bytes 393224 | tf_op jit(solution)/shard_map/ppermute | solution.py:12
  124.3 1.3 collective-permute-start.11
  125.6 2.3 convolution_convert_fusion.12
  127.9 1.0 copy.229
  128.9 1.1 convert.6
  130.5 1.1 copy.221
  131.6 1.1 copy.222
  132.7 1.1 copy.223
  133.9 1.8 copy.224
  135.7 5.6 %stack.51 = bf16[6,128,512]{2,0,1:T(8,128)(2,1)} concatenate(bf16[1,128,512]{2,0,1:T(2,128)(2,1)S(1)} %copy.219, bf16[1,128,512]{2,0,1:T(2,128)(2,1)S(1)} %copy.220, bf16[1,128,512]{2,0,1:T(2,128)(2,1)S(1)} %copy.221, bf16[1,128,512]{2,0,1:T(2,128)(2,1)S(1)} %copy.222, bf16[1,128,512]{2,0,1:T(2,128)(2,1)S(1)} %copy.223, bf16[1,128,512]{2,0,1:T(2,128)(2,1)} %copy.224), dimensions={0} | concatenate | bytes 1572864 | tf_op jit(solution)/shard_map/stack | solution.py:84
  141.3 2.9 convolution_add_fusion
  144.2 1.3 copy.225
  145.5 237.8 %all-reduce.12.cloned.1.call-done = (f32[786432]{0:T(1024)}, f32[262144]{0:T(1024)}, f32[524288]{0:T(1024)}, f32[262144]{0:T(1024)}) async-done(((f32[786432]{0:T(1024)}, f32[262144]{0:T(1024)}, f32[524288]{0:T(1024)}, f32[262144]{0:T(1024)}), (f32[786432]{0:T(1024)}, f32[262144]{0:T(1024)}, f32[524288]{0:T(1024)}, f32[262144]{0:T(1024)})) %all-reduce.12.cloned.1.call-update) | async-done | bytes 7340048
  383.3 1.3 dynamic-slice.1
  384.6 1.3 dynamic-slice.3
  385.8 1.3 dynamic-slice
  387.1 1.3 dynamic-slice.2
  (114 shorter events, 15.8 us)
Async XLA Ops:
  7.2 54.3 %copy-start = (bf16[512,512]{1,0:T(8,128)(2,1)S(1)}, bf16[512,512]{1,0:T(8,128)(2,1)}, u32[]{:S(2)}) copy-start(bf16[512,512]{1,0:T(8,128)(2,1)} %param.19) | copy-start | bytes 1572868
  7.2 376.1 %all-reduce.12.cloned.1.call-start = ((), (), s32[]{:S(2)}) async-start(), calls=%async_computation | async-start | bytes 14680064
  8.9 17.8 %copy-start.3 = (bf16[1024,512]{1,0:T(8,128)(2,1)S(1)}, bf16[1024,512]{1,0:T(8,128)(2,1)}, u32[]{:S(2)}) copy-start(bf16[1024,512]{1,0:T(8,128)(2,1)} %param.13) | copy-start | bytes 3145732
  8.9 17.8 %copy-start.11 = (bf16[1536,512]{1,0:T(8,128)(2,1)S(1)}, bf16[1536,512]{1,0:T(8,128)(2,1)}, u32[]{:S(2)}) copy-start(bf16[1536,512]{1,0:T(8,128)(2,1)} %param.18) | copy-start | bytes 4718596
  10.1 20.7 %collective-permute-start = (bf16[128,512]{1,0:T(8,128)(2,1)S(1)}, bf16[128,512]{1,0:T(8,128)(2,1)S(1)}, u32[]{:S(2)}, u32[]{:S(2)}) collective-permute-start(bf16[128,512]{1,0:T(8,128)(2,1)S(1)} %bitcast.163), channel_id=1, source_target_pairs={{0,16},{16,32},{32,48},{48,64},{64,80},{80,96},{96,112},{1,17},{17... | collective-permute-start | bytes 393224 | tf_op jit(solution)/shard_map/ppermute | solution.py:12
  13.3 24.3 %collective-permute-start.1 = (bf16[128,512]{1,0:T(8,128)(2,1)S(1)}, bf16[128,512]{1,0:T(8,128)(2,1)S(1)}, u32[]{:S(2)}, u32[]{:S(2)}) collective-permute-start(bf16[128,512]{1,0:T(8,128)(2,1)S(1)} %bitcast.158), channel_id=1, source_target_pairs={{16,0},{32,16},{48,32},{64,48},{80,64},{96,80},{112,96},{17,1},{33... | collective-permute-start | bytes 393224 | tf_op jit(solution)/shard_map/ppermute | solution.py:12
  18.2 20.3 %collective-permute-start.2 = (bf16[128,512]{1,0:T(8,128)(2,1)}, bf16[128,512]{1,0:T(8,128)(2,1)}, u32[]{:S(2)}, u32[]{:S(2)}) collective-permute-start(bf16[128,512]{1,0:T(8,128)(2,1)} %bitcast.133), channel_id=1, source_target_pairs={{0,1},{1,2},{2,3},{3,4},{4,5},{5,6},{6,7},{7,8},{8,9},{9,10},{10,1... | collective-permute-start | bytes 393224 | tf_op jit(solution)/shard_map/ppermute | solution.py:12
  20.8 8.0 %copy-start.2 = (bf16[512,512]{1,0:T(8,128)(2,1)S(1)}, bf16[512,512]{1,0:T(8,128)(2,1)}, u32[]{:S(2)}) copy-start(bf16[512,512]{1,0:T(8,128)(2,1)} %param.12) | copy-start | bytes 1572868
  20.8 19.5 %collective-permute-start.3 = (bf16[128,512]{1,0:T(8,128)(2,1)}, bf16[128,512]{1,0:T(8,128)(2,1)}, u32[]{:S(2)}, u32[]{:S(2)}) collective-permute-start(bf16[128,512]{1,0:T(8,128)(2,1)} %bitcast.132), channel_id=1, source_target_pairs={{1,0},{2,1},{3,2},{4,3},{5,4},{6,5},{7,6},{8,7},{9,8},{10,9},{11,1... | collective-permute-start | bytes 393224 | tf_op jit(solution)/shard_map/ppermute | solution.py:12
  22.9 19.3 %collective-permute-start.4 = (bf16[128,512]{1,0:T(8,128)(2,1)}, bf16[128,512]{1,0:T(8,128)(2,1)}, u32[]{:S(2)}, u32[]{:S(2)}) collective-permute-start(bf16[128,512]{1,0:T(8,128)(2,1)} %bitcast.131), channel_id=1, source_target_pairs={{0,128},{1,129},{2,130},{3,131},{4,132},{5,133},{6,134},{7,135},{8... | collective-permute-start | bytes 393224 | tf_op jit(solution)/shard_map/ppermute | solution.py:12
  28.8 3.6 copy-start.12
  30.8 13.1 %collective-permute-start.5 = (bf16[128,512]{1,0:T(8,128)(2,1)}, bf16[128,512]{1,0:T(8,128)(2,1)}, u32[]{:S(2)}, u32[]{:S(2)}) collective-permute-start(bf16[128,512]{1,0:T(8,128)(2,1)} %bitcast.130), channel_id=1, source_target_pairs={{128,0},{129,1},{130,2},{131,3},{132,4},{133,5},{134,6},{135,7},{1... | collective-permute-start | bytes 393224 | tf_op jit(solution)/shard_map/ppermute | solution.py:12
  33.7 2.7 copy-start.27
  33.7 2.9 copy-start.28
  36.4 31.9 %copy-start.6 = (bf16[512,512]{0,1:T(8,128)(2,1)}, bf16[512,512]{0,1:T(8,128)(2,1)S(1)}, u32[]{:S(2)}) copy-start(bf16[512,512]{0,1:T(8,128)(2,1)S(1)} %copy.213) | copy-start | bytes 1572868
  45.7 13.1 %copy-start.21 = (bf16[4,2,128,128]{3,2,1,0:T(8,128)(2,1)S(1)}, bf16[4,2,128,128]{3,2,1,0:T(8,128)(2,1)}, u32[]{:S(2)}) copy-start(bf16[4,2,128,128]{3,2,1,0:T(8,128)(2,1)} %param.14) | copy-start | bytes 786436
  56.6 3.1 copy-start.5
  56.6 3.1 copy-start.10
  64.2 1.2 copy-start.8
  64.2 1.5 copy-start.13
  64.6 1.6 copy-start.29
  69.0 11.6 %copy-start.17 = (bf16[512,512]{1,0:T(8,128)(2,1)}, bf16[512,512]{1,0:T(8,128)(2,1)S(1)}, u32[]{:S(2)}) copy-start(bf16[512,512]{1,0:T(8,128)(2,1)S(1)} %fusion.29) | copy-start | bytes 1572868
  69.0 1.4 copy-start.9
  72.9 1.3 copy-start.4
  79.3 2.5 copy-start.7
  83.7 2.7 copy-start.15
  87.8 2.5 copy-start.22
  90.3 1.3 copy-start.20
  90.3 1.3 copy-start.25
  91.9 1.9 copy-start.23
  101.1 5.8 %copy-start.14 = (bf16[1024,512]{1,0:T(8,128)(2,1)S(1)}, bf16[1024,512]{1,0:T(8,128)(2,1)}, u32[]{:S(2)}) copy-start(bf16[1024,512]{1,0:T(8,128)(2,1)} %param.20) | copy-start | bytes 3145732
  101.2 5.8 %copy-start.18 = (bf16[512,512]{1,0:T(8,128)(2,1)S(1)}, bf16[512,512]{1,0:T(8,128)(2,1)}, u32[]{:S(2)}) copy-start(bf16[512,512]{1,0:T(8,128)(2,1)} %copy-done.17) | copy-start | bytes 1572868
  101.2 5.8 %copy-start.24 = (bf16[512,512]{1,0:T(8,128)(2,1)S(1)}, bf16[512,512]{1,0:T(8,128)(2,1)}, u32[]{:S(2)}) copy-start(bf16[512,512]{1,0:T(8,128)(2,1)} %param.22) | copy-start | bytes 1572868
  102.4 23.1 %copy-start.19 = (bf16[4,128,512]{2,1,0:T(8,128)(2,1)S(1)}, bf16[4,128,512]{2,1,0:T(8,128)(2,1)}, u32[]{:S(2)}) copy-start(bf16[4,128,512]{2,1,0:T(8,128)(2,1)} %reduce_sum.115) | copy-start | bytes 1572868
  102.4 21.8 %collective-permute-start.6 = (bf16[128,512]{1,0:T(8,128)(2,1)S(1)}, bf16[128,512]{1,0:T(8,128)(2,1)S(1)}, u32[]{:S(2)}, u32[]{:S(2)}) collective-permute-start(bf16[128,512]{1,0:T(8,128)(2,1)S(1)} %bitcast.164), channel_id=1, source_target_pairs={{0,16},{16,32},{32,48},{48,64},{64,80},{80,96},{96,112},{1,17},{17... | collective-permute-start | bytes 393224 | tf_op jit(solution)/shard_map/ppermute | solution.py:12
  107.4 20.5 %copy-start.16 = (bf16[512,512]{0,1:T(8,128)(2,1)S(1)}, bf16[512,512]{0,1:T(8,128)(2,1)}, u32[]{:S(2)}) copy-start(bf16[512,512]{0,1:T(8,128)(2,1)} %get-tuple-element.87) | copy-start | bytes 1572868
  107.5 22.8 %collective-permute-start.7 = (bf16[128,512]{1,0:T(8,128)(2,1)S(1)}, bf16[128,512]{1,0:T(8,128)(2,1)S(1)}, u32[]{:S(2)}, u32[]{:S(2)}) collective-permute-start(bf16[128,512]{1,0:T(8,128)(2,1)S(1)} %bitcast.161), channel_id=1, source_target_pairs={{16,0},{32,16},{48,32},{64,48},{80,64},{96,80},{112,96},{17,1},{33... | collective-permute-start | bytes 393224 | tf_op jit(solution)/shard_map/ppermute | solution.py:12
  111.3 19.2 %collective-permute-start.8 = (bf16[128,512]{1,0:T(8,128)(2,1)}, bf16[128,512]{1,0:T(8,128)(2,1)}, u32[]{:S(2)}, u32[]{:S(2)}) collective-permute-start(bf16[128,512]{1,0:T(8,128)(2,1)} %bitcast.127), channel_id=1, source_target_pairs={{0,1},{1,2},{2,3},{3,4},{4,5},{5,6},{6,7},{7,8},{8,9},{9,10},{10,1... | collective-permute-start | bytes 393224 | tf_op jit(solution)/shard_map/ppermute | solution.py:12
  116.3 15.3 %collective-permute-start.9 = (bf16[128,512]{1,0:T(8,128)(2,1)}, bf16[128,512]{1,0:T(8,128)(2,1)}, u32[]{:S(2)}, u32[]{:S(2)}) collective-permute-start(bf16[128,512]{1,0:T(8,128)(2,1)} %bitcast.126), channel_id=1, source_target_pairs={{1,0},{2,1},{3,2},{4,3},{5,4},{6,5},{7,6},{8,7},{9,8},{10,9},{11,1... | collective-permute-start | bytes 393224 | tf_op jit(solution)/shard_map/ppermute | solution.py:12
  118.3 14.5 %collective-permute-start.10 = (bf16[128,512]{1,0:T(8,128)(2,1)}, bf16[128,512]{1,0:T(8,128)(2,1)}, u32[]{:S(2)}, u32[]{:S(2)}) collective-permute-start(bf16[128,512]{1,0:T(8,128)(2,1)} %bitcast.125), channel_id=1, source_target_pairs={{0,128},{1,129},{2,130},{3,131},{4,132},{5,133},{6,134},{7,135},{8... | collective-permute-start | bytes 393224 | tf_op jit(solution)/shard_map/ppermute | solution.py:12
  124.3 9.6 %collective-permute-start.11 = (bf16[128,512]{1,0:T(8,128)(2,1)}, bf16[128,512]{1,0:T(8,128)(2,1)}, u32[]{:S(2)}, u32[]{:S(2)}) collective-permute-start(bf16[128,512]{1,0:T(8,128)(2,1)} %bitcast.124), channel_id=1, source_target_pairs={{128,0},{129,1},{130,2},{131,3},{132,4},{133,5},{134,6},{135,7},{1... | collective-permute-start | bytes 393224 | tf_op jit(solution)/shard_map/ppermute | solution.py:12
  130.5 10.8 %copy-start.26 = (s32[1,6]{1,0:T(1,128)S(1)}, s32[1,6]{1,0:T(1,128)}, u32[]{:S(2)}) copy-start(s32[1,6]{1,0:T(1,128)} %param.17) | copy-start | bytes 76
  141.3 247.1 %copy-start.1 = (bf16[512,512]{1,0:T(8,128)(2,1)S(1)}, bf16[512,512]{1,0:T(8,128)(2,1)}, u32[]{:S(2)}) copy-start(bf16[512,512]{1,0:T(8,128)(2,1)} %param.19) | copy-start | bytes 1572868
Sparse Core Ops, SparseCore 0:
  95.2 288.0 all-reduce.11
where the time goes:
time: 398 us; the launch traced here: 395 us
  waiting for transfers between devices  238 us (60%)
  local copies, waits for them, and re-layouts  60.1 us (15%)
  matrix products  36.8 us (9%)
  starting transfers between devices  35.9 us (9%)
  between operations  14.7 us (4%)
  other arithmetic  10.1 us (3%)
    unnamed x2, waiting for transfers between devices  238 us
    ppermute x12, starting transfers between devices, passed_along(): return lax.ppermute(block, axis, route)  35.9 us
    unnamed x84, local copies, waits for them, and re-layouts  22.2 us
    another operation x13, local copies, waits for them, and re-layouts, swap_faces(): jnp.stack([across_rows(face_blocks[1], 1), across_rows(face_blocks[0], -1...  20.2 us
    concatenate x1, local copies, waits for them, and re-layouts, edge_part(): extended = jnp.concatenate([node_blocks, received], axis=0)  10.9 us
  transfers between devices with their start and end apart: 13, of which 1 were waited for; matrix products, arithmetic and copies ran while one was open for 12% of the time, Pallas kernels for 0%

commit v1 on v0

--- a/solution.py
+++ b/solution.py
@@ -10,6 +10,27 @@
     devices = range(lax.axis_size(axis))
     route = [(i - distance, i) for i in devices if i - distance in devices]
     return lax.ppermute(block, axis, route)
+
+
+INDEX_BITS = (("segment", 0), ("gx", 2), ("gx", 1), ("gx", 0), ("gy", 3), ("gy", 2), ("gy", 1), ("gy", 0))
+EDGE_IN_ORDER = (7, 0, 6, 2, 5, 3, 1, 4)
+EDGE_OUT_ORDER = (7, 2, 0, 6, 1, 5, 3, 4)
+NODE_IN_ORDER = (7, 6, 2, 0, 3, 5, 4, 1)
+NODE_OUT_ORDER = (7, 2, 0, 6, 1, 5, 3, 4)
+
+
+def halving_scatter(flat, order):
+    devices = 1 << len(INDEX_BITS)
+    share = flat.shape[0] // devices
+    parts = flat.reshape((2,) * len(INDEX_BITS) + (share,)).transpose(tuple(order) + (len(INDEX_BITS),))
+    for position in order:
+        axis, bit = INDEX_BITS[position]
+        side = (lax.axis_index(axis) >> bit) & 1
+        route = [(j, j ^ (1 << bit)) for j in range(lax.axis_size(axis))]
+        keep = lax.dynamic_index_in_dim(parts, side, 0, keepdims=False)
+        send = lax.dynamic_index_in_dim(parts, 1 - side, 0, keepdims=False)
+        parts = keep + lax.ppermute(send, axis, route)
+    return parts
 
 
 def layer_norm(values):
@@ -148,10 +169,10 @@
     )
     edge_terms = (grad_ei.astype(jnp.float32).reshape(-1), grad_eo.astype(jnp.float32).reshape(-1))
     shares = (
-        lax.psum_scatter(edge_terms[0], ("segment", "gx", "gy"), scatter_dimension=0, tiled=True),
-        lax.psum_scatter(edge_terms[1], ("segment", "gx", "gy"), scatter_dimension=0, tiled=True),
-        lax.psum_scatter(node_terms[0], ("segment", "gx", "gy"), scatter_dimension=0, tiled=True),
-        lax.psum_scatter(node_terms[1], ("segment", "gx", "gy"), scatter_dimension=0, tiled=True),
+        halving_scatter(edge_terms[0], EDGE_IN_ORDER),
+        halving_scatter(edge_terms[1], EDGE_OUT_ORDER),
+        halving_scatter(node_terms[0], NODE_IN_ORDER),
+        halving_scatter(node_terms[1], NODE_OUT_ORDER),
     )
     return (
         outputs[0],

time: 398 us -> 299 us (0.75)
  waiting for transfers between devices: 238 us -> 42.4 us
  starting transfers between devices: 35.9 us -> 105 us
  local copies, waits for them, and re-layouts: 60.1 us -> 87.7 us
  between operations: 14.7 us -> 1.82 us
  other arithmetic: 10.1 us -> 21.8 us
    unnamed x2 -> x0, waiting for transfers between devices: 238 us -> none
    ppermute x0 -> x32, starting transfers between devices: none -> 71.2 us  [halving_scatter(): parts = keep + lax.ppermute(send, axis, route)]
    ppermute x0 -> x32, waiting for transfers between devices: none -> 42.4 us  [halving_scatter(): parts = keep + lax.ppermute(send, axis, route)]
    another operation x0 -> x7, local copies, waits for them, and re-layouts: none -> 29.4 us
    add x0 -> x32, other arithmetic: none -> 12.1 us  [halving_scatter(): parts = keep + lax.ppermute(send, axis, route)]
    unnamed x84 -> x105, local copies, waits for them, and re-layouts: 22.2 us -> 16 us
  transfers between devices with their start and end apart: 13 -> 44, of which waited for: 1 -> 13; matrix products, arithmetic and copies ran while one was open for 12% -> 28% of each run, Pallas kernels for 0% -> 0%
where the time goes in v1:
time: 299 us; the launch traced here: 293 us
  starting transfers between devices  105 us (35%)
  local copies, waits for them, and re-layouts  87.7 us (29%)
  waiting for transfers between devices  42.4 us (14%)
  matrix products  34.6 us (12%)
  other arithmetic  21.8 us (7%)
    ppermute x32, starting transfers between devices, halving_scatter(): parts = keep + lax.ppermute(send, axis, route)  71.2 us
    ppermute x32, waiting for transfers between devices, halving_scatter(): parts = keep + lax.ppermute(send, axis, route)  42.4 us
    ppermute x12, starting transfers between devices, passed_along(): return lax.ppermute(block, axis, route)  33.8 us
    another operation x13, local copies, waits for them, and re-layouts, swap_faces(): jnp.stack([across_rows(face_blocks[1], 1), across_rows(face_blocks[0], -1...  22.5 us
    another operation x3, local copies, waits for them, and re-layouts  17.1 us
    unnamed x105, local copies, waits for them, and re-layouts  16 us
    another operation x4, local copies, waits for them, and re-layouts, halving_scatter(): flat.reshape((2,) * len(INDEX_BITS) + (share,))  12.3 us
    add x32, other arithmetic, halving_scatter(): parts = keep + lax.ppermute(send, axis, route)  12.1 us
  transfers between devices with their start and end apart: 44, of which 13 were waited for; matrix products, arithmetic and copies ran while one was open for 28% of the time, Pallas kernels for 0%

profile of v1, /device:TPU:16, one launch (start us, length us, event | category | flops | bytes accessed | tf_op | source)
XLA Modules:
  0.0 293.4 jit_solution(11104689070390938266)
XLA Ops:
  3.6 3.2 %collective-permute-start = (bf16[128,512]{1,0:T(8,128)(2,1)S(1)}, bf16[128,512]{1,0:T(8,128)(2,1)S(1)}, u32[]{:S(2)}, u32[]{:S(2)}) collective-permute-start(bf16[128,512]{1,0:T(8,128)(2,1)S(1)} %bitcast.313), channel_id=1, source_target_pairs={{0,16},{16,32},{32,48},{48,64},{64,80},{80,96},{96,112},{1,17},{17... | collective-permute-start | bytes 393224 | tf_op jit(solution)/shard_map/ppermute | solution.py:12
  6.8 4.2 %collective-permute-start.1 = (bf16[128,512]{1,0:T(8,128)(2,1)S(1)}, bf16[128,512]{1,0:T(8,128)(2,1)S(1)}, u32[]{:S(2)}, u32[]{:S(2)}) collective-permute-start(bf16[128,512]{1,0:T(8,128)(2,1)S(1)} %bitcast.305), channel_id=1, source_target_pairs={{16,0},{32,16},{48,32},{64,48},{80,64},{96,80},{112,96},{17,1},{33... | collective-permute-start | bytes 393224 | tf_op jit(solution)/shard_map/ppermute | solution.py:12
  11.6 1.9 collective-permute-start.2
  16.3 3.8 %collective-permute-start.4 = (bf16[128,512]{1,0:T(8,128)(2,1)}, bf16[128,512]{1,0:T(8,128)(2,1)}, u32[]{:S(2)}, u32[]{:S(2)}) collective-permute-start(bf16[128,512]{1,0:T(8,128)(2,1)} %bitcast.273), channel_id=1, source_target_pairs={{0,128},{1,129},{2,130},{3,131},{4,132},{5,133},{6,134},{7,135},{8... | collective-permute-start | bytes 393224 | tf_op jit(solution)/shard_map/ppermute | solution.py:12
  20.1 2.0 fusion.38
  32.2 1.8 copy.206
  34.0 1.8 copy.207
  35.8 1.8 copy.208
  37.6 1.8 copy.209
  39.4 10.9 %concatenate.3 = bf16[10,128,512]{2,0,1:T(8,128)(2,1)} concatenate(bf16[4,128,512]{2,0,1:T(4,128)(2,1)} %copy.203, bf16[1,128,512]{2,0,1:T(2,128)(2,1)} %copy.204, bf16[1,128,512]{2,0,1:T(2,128)(2,1)} %copy.205, bf16[1,128,512]{2,0,1:T(2,128)(2,1)} %copy.206, bf16[1,128,512]{2,0,1:T(2,128)(2,1)} %copy.207, bf16[1,128,512]{2,0,1:T(2,128)(2,1)} %copy.208, bf16[1,128,512]{2,0,1:T(2,128)(2,1)} %copy.209), dimensions={0} | concatenate | bytes 2621440 | tf_op jit(solution)/shard_map/jvp()/concatenate | solution.py:47
  50.4 2.2 convolution_convert_fusion.5
  61.6 1.8 fusion.18
  68.7 1.8 fusion.72
  70.5 2.0 fusion.15
  78.7 2.9 reshape.123
  81.6 2.9 reshape.121
  84.5 5.5 %constant_dynamic-slice_fusion.8 = (f32[2,2,2,2,2,2,2,1,1024]{8,7,6,5,4,3,2,1,0:T(1,128)}, f32[1,2,2,2,2,2,2,2,1024]{8,0,3,5,7,6,1,4,2:T(1,128)S(1)}, f32[1,2,2,...) fusion(f32[2,2,2,2,2,2,2,2,1024]{8,7,6,5,4,3,2,1,0:T(2,128)} %reshape.123, s32[]{:T(128)S(6)} %select_n.120, ...), kind=kLoop, calls=%fused_computation.163 | loop fusion | bytes 4194312 | tf_op jit(solution)/shard_map/dynamic-slice.6
  95.4 2.4 collective-permute-start.20
  97.9 2.2 convolution_convert_fusion
  100.3 2.9 reshape.122
  103.2 1.8 add_convert_fusion.1
  105.0 3.7 %reshape.120 = f32[2,2,2,2,2,2,2,2,3072]{8,7,6,5,4,3,2,1,0:T(2,128)} reshape(f32[1536,512]{1,0:T(8,128)S(1)} %add_convert_fusion.1) | data formatting | bytes 6291456 | tf_op jit(solution)/shard_map/reshape;reshape | solution.py:25
  108.7 8.0 %constant_dynamic-slice_fusion.33 = (f32[2,2,2,2,2,2,2,1,3072]{8,7,6,5,4,3,2,1,0:T(1,128)}, f32[1,2,2,2,2,2,2,2,3072]{8,0,2,4,7,5,3,6,1:T(1,128)}) fusion(f32[2,2,2,2,2,2,2,2,3072]{8,7,6,5,4,3,2,1,0:T(2,128)} %reshape.120, s32[]{:T(128)S(6)} %select_n.120, s32[]{:T(128)S(6)} %select_n.121), kind=kLoop, calls=%fused_computation.188 | loop fusion | bytes 6291464 | tf_op jit(solution)/shard_map/dynamic-slice
  118.0 4.4 %collective-permute-start.6 = (bf16[128,512]{1,0:T(8,128)(2,1)S(1)}, bf16[128,512]{1,0:T(8,128)(2,1)S(1)}, u32[]{:S(2)}, u32[]{:S(2)}) collective-permute-start(bf16[128,512]{1,0:T(8,128)(2,1)S(1)} %bitcast.314), channel_id=1, source_target_pairs={{0,16},{16,32},{32,48},{48,64},{64,80},{80,96},{96,112},{1,17},{17... | collective-permute-start | bytes 393224 | tf_op jit(solution)/shard_map/ppermute | solution.py:12
  122.4 3.0 %collective-permute-start.7 = (bf16[128,512]{1,0:T(8,128)(2,1)S(1)}, bf16[128,512]{1,0:T(8,128)(2,1)S(1)}, u32[]{:S(2)}, u32[]{:S(2)}) collective-permute-start(bf16[128,512]{1,0:T(8,128)(2,1)S(1)} %bitcast.312), channel_id=1, source_target_pairs={{16,0},{32,16},{48,32},{64,48},{80,64},{96,80},{112,96},{17,1},{33... | collective-permute-start | bytes 393224 | tf_op jit(solution)/shard_map/ppermute | solution.py:12
  125.4 1.9 collective-permute-start.8
  127.3 3.6 %constant_dynamic-slice_fusion.17 = (f32[2,2,2,2,2,2,2,1,2048]{8,7,6,5,4,3,2,1,0:T(1,128)}, f32[1,2,2,2,2,2,2,2,2048]{8,0,1,5,6,4,2,7,3:T(1,128)}) fusion(f32[2,2,2,2,2,2,2,2,2048]{8,7,6,5,4,3,2,1,0:T(2,128)S(1)} %copy-done.7, s32[]{:T(128)S(6)} %select_n.120, s32[]{:T(128)S(6)} %select_n.121), kind=kLoop, calls=%fused_computation.172 | loop fusion | bytes 4194312 | tf_op jit(solution)/shard_map/dynamic-slice.4
  133.5 5.5 %collective-permute-start.10 = (bf16[128,512]{1,0:T(8,128)(2,1)}, bf16[128,512]{1,0:T(8,128)(2,1)}, u32[]{:S(2)}, u32[]{:S(2)}) collective-permute-start(bf16[128,512]{1,0:T(8,128)(2,1)} %bitcast.267), channel_id=1, source_target_pairs={{0,128},{1,129},{2,130},{3,131},{4,132},{5,133},{6,134},{7,135},{8... | collective-permute-start | bytes 393224 | tf_op jit(solution)/shard_map/ppermute | solution.py:12
  140.6 2.3 convolution_convert_fusion.12
  145.1 2.9 copy.330
  148.0 2.0 copy.329
  152.1 3.2 %collective-permute-start.28 = (f32[2,2,2,2,2,2,2,2048]{7,0,4,5,3,1,6,2:T(2,128)}, f32[2,2,2,2,2,2,2,2048]{7,0,4,5,3,1,6,2:T(2,128)}, u32[]{:S(2)}, u32[]{:S(2)}) collective-permute-start(f32[2,2,2,2,2,2,2,2048]{7,0,4,5,3,1,6,2:T(2,128)} %bitcast.261), channel_id=1, source_target_pairs={{0,1},{1,0},{2,3},{3,2},{4,5},{5,4},{6,7},{7,6},{8,9},{9,8},{10,11... | collective-permute-start | bytes 3145736 | tf_op jit(solution)/shard_map/ppermute | solution.py:32
  155.3 1.8 copy.221
  157.1 1.8 copy.222
  158.9 1.8 copy.223
  160.7 5.9 %stack.51 = bf16[6,128,512]{2,0,1:T(8,128)(2,1)} concatenate(bf16[1,128,512]{2,0,1:T(2,128)(2,1)S(1)} %copy.218, bf16[1,128,512]{2,0,1:T(2,128)(2,1)} %copy.219, bf16[1,128,512]{2,0,1:T(2,128)(2,1)} %copy.220, bf16[1,128,512]{2,0,1:T(2,128)(2,1)} %copy.221, bf16[1,128,512]{2,0,1:T(2,128)(2,1)} %copy.222, bf16[1,128,512]{2,0,1:T(2,128)(2,1)} %copy.223), dimensions={0} | concatenate | bytes 1572864 | tf_op jit(solution)/shard_map/stack | solution.py:105
  171.8 5.6 %collective-permute-done.21 = f32[2,2,2,2,2,2,1024]{6,1,3,5,4,2,0:T(2,128)S(1)} collective-permute-done((f32[2,2,2,2,2,2,1024]{6,1,3,5,4,2,0:T(2,128)S(1)}, f32[2,2,2,2,2,2,1024]{6,1,3,5,4,2,0:T(2,128)S(1)}, u32[]{:S(2)}, u32[]{:S(2)}) %collective-permute-start.21) | collective-permute-done | bytes 262176 | tf_op jit(solution)/shard_map/ppermute | solution.py:32
  177.6 3.1 %collective-permute-start.22 = (f32[2,2,2,2,2,1024]{5,0,2,4,3,1:T(2,128)S(1)}, f32[2,2,2,2,2,1024]{5,0,2,4,3,1:T(2,128)S(1)}, u32[]{:S(2)}, u32[]{:S(2)}) collective-permute-start(f32[2,2,2,2,2,1024]{5,0,2,4,3,1:T(2,128)S(1)} %dynamic-slice_bitcast_fusion.11), channel_id=1, source_target_pairs={{0,128},{128,0},{1,129},{129,1},{2,130},{130,2},{3,131},{131,3},{4... | collective-permute-start | bytes 393224 | tf_op jit(solution)/shard_map/ppermute | solution.py:32
  180.6 1.9 collective-permute-done.37
  182.7 3.1 %collective-permute-start.38 = (f32[2,2,2,2,2,1024]{5,0,2,4,3,1:T(2,128)S(1)}, f32[2,2,2,2,2,1024]{5,0,2,4,3,1:T(2,128)S(1)}, u32[]{:S(2)}, u32[]{:S(2)}) collective-permute-start(f32[2,2,2,2,2,1024]{5,0,2,4,3,1:T(2,128)S(1)} %dynamic-slice_bitcast_fusion.9), channel_id=1, source_target_pairs={{0,128},{128,0},{1,129},{129,1},{2,130},{130,2},{3,131},{131,3},{4... | collective-permute-start | bytes 393224 | tf_op jit(solution)/shard_map/ppermute | solution.py:32
  186.0 2.3 collective-permute-start.23
  189.3 1.9 collective-permute-start.39
  191.3 3.1 %collective-permute-start.24 = (f32[2,2,2,1024]{3,0,2,1:T(2,128)S(1)}, f32[2,2,2,1024]{3,0,2,1:T(2,128)S(1)}, u32[]{:S(2)}, u32[]{:S(2)}) collective-permute-start(f32[2,2,2,1024]{3,0,2,1:T(2,128)S(1)} %dynamic-slice_bitcast_fusion.15), channel_id=1, source_target_pairs={{0,64},{16,80},{32,96},{48,112},{64,0},{80,16},{96,32},{112,48},{1... | collective-permute-start | bytes 98312 | tf_op jit(solution)/shard_map/ppermute | solution.py:32
  194.5 2.4 collective-permute-start.40
  197.2 5.6 %collective-permute-start.25 = (f32[2,2,1024]{2,1,0:T(2,128)S(1)}, f32[2,2,1024]{2,1,0:T(2,128)S(1)}, u32[]{:S(2)}, u32[]{:S(2)}) collective-permute-start(f32[2,2,1024]{2,1,0:T(2,128)S(1)} %bitcast.325), channel_id=1, source_target_pairs={{0,4},{1,5},{2,6},{3,7},{4,0},{5,1},{6,2},{7,3},{8,12},{9,13},{10,... | collective-permute-start | bytes 49160 | tf_op jit(solution)/shard_map/ppermute | solution.py:32
  202.9 3.5 %collective-permute-start.41 = (f32[2,2,1024]{2,1,0:T(2,128)S(1)}, f32[2,2,1024]{2,1,0:T(2,128)S(1)}, u32[]{:S(2)}, u32[]{:S(2)}) collective-permute-start(f32[2,2,1024]{2,1,0:T(2,128)S(1)} %bitcast.327), channel_id=1, source_target_pairs={{0,4},{1,5},{2,6},{3,7},{4,0},{5,1},{6,2},{7,3},{8,12},{9,13},{10,... | collective-permute-start | bytes 49160 | tf_op jit(solution)/shard_map/ppermute | solution.py:32
  206.4 2.5 collective-permute-start.26
  210.6 2.0 fusion.28
  214.1 1.9 collective-permute-start.29
  216.0 5.2 %collective-permute-start.27 = (f32[1024]{0:T(1024)S(1)}, f32[1024]{0:T(1024)S(1)}, u32[]{:S(2)}, u32[]{:S(2)}) collective-permute-start(f32[1024]{0:T(1024)S(1)} %bitcast.330), channel_id=1, source_target_pairs={{0,8},{1,9},{2,10},{3,11},{4,12},{5,13},{6,14},{7,15},{8,0},{9,1},... | collective-permute-start | bytes 12296 | tf_op jit(solution)/shard_map/ppermute | solution.py:32
  221.2 3.3 %collective-permute-done.29 = f32[2,2,2,2,2,2,2048]{6,3,4,2,0,5,1:T(2,128)S(1)} collective-permute-done((f32[2,2,2,2,2,2,2048]{6,3,4,2,0,5,1:T(2,128)S(1)}, f32[2,2,2,2,2,2,2048]{6,3,4,2,0,5,1:T(2,128)S(1)}, u32[]{:S(2)}, u32[]{:S(2)}) %collective-permute-start.29) | collective-permute-done | bytes 524320 | tf_op jit(solution)/shard_map/ppermute | solution.py:32
  225.9 2.5 fusion.7
  228.5 2.8 collective-permute-done.30
  231.5 2.4 collective-permute-start.31
  234.1 5.5 %collective-permute-start.43 = (f32[1024]{0:T(1024)S(1)}, f32[1024]{0:T(1024)S(1)}, u32[]{:S(2)}, u32[]{:S(2)}) collective-permute-start(f32[1024]{0:T(1024)S(1)} %bitcast.331), channel_id=1, source_target_pairs={{0,8},{1,9},{2,10},{3,11},{4,12},{5,13},{6,14},{7,15},{8,0},{9,1},... | collective-permute-start | bytes 12296 | tf_op jit(solution)/shard_map/ppermute | solution.py:32
  240.7 8.9 %collective-permute-done.13 = f32[2,2,2,2,2,2,3072]{6,0,2,5,3,1,4:T(2,128)S(1)} collective-permute-done((f32[2,2,2,2,2,2,3072]{6,0,2,5,3,1,4:T(2,128)S(1)}, f32[2,2,2,2,2,2,3072]{6,0,2,5,3,1,4:T(2,128)S(1)}, u32[]{:S(2)}, u32[]{:S(2)}) %collective-permute-start.13) | collective-permute-done | bytes 786464 | tf_op jit(solution)/shard_map/ppermute | solution.py:32
  252.3 1.8 collective-permute-start.33
  254.1 5.3 %collective-permute-done.14 = f32[2,2,2,2,2,3072]{5,1,4,2,0,3:T(2,128)S(1)} collective-permute-done((f32[2,2,2,2,2,3072]{5,1,4,2,0,3:T(2,128)S(1)}, f32[2,2,2,2,2,3072]{5,1,4,2,0,3:T(2,128)S(1)}, u32[]{:S(2)}, u32[]{:S(2)}) %collective-permute-start.14) | collective-permute-done | bytes 393248 | tf_op jit(solution)/shard_map/ppermute | solution.py:32
  260.1 5.4 %collective-permute-done.15 = f32[2,2,2,2,3072]{4,0,3,1,2:T(2,128)S(1)} collective-permute-done((f32[2,2,2,2,3072]{4,0,3,1,2:T(2,128)S(1)}, f32[2,2,2,2,3072]{4,0,3,1,2:T(2,128)S(1)}, u32[]{:S(2)}, u32[]{:S(2)}) %collective-permute-start.15) | collective-permute-done | bytes 196640 | tf_op jit(solution)/shard_map/ppermute | solution.py:32
  265.8 2.9 collective-permute-start.16
  270.4 2.1 collective-permute-done.16
  273.7 2.8 collective-permute-done.34
  278.3 2.0 collective-permute-start.18
  283.8 4.5 %collective-permute-start.19 = (f32[3072]{0:T(1024)S(1)}, f32[3072]{0:T(1024)S(1)}, u32[]{:S(2)}, u32[]{:S(2)}) collective-permute-start(f32[3072]{0:T(1024)S(1)} %bitcast.328), channel_id=1, source_target_pairs={{0,8},{1,9},{2,10},{3,11},{4,12},{5,13},{6,14},{7,15},{8,0},{9,1},... | collective-permute-start | bytes 36872 | tf_op jit(solution)/shard_map/ppermute | solution.py:32
  (263 shorter events, 81.8 us)
Async XLA Ops:
  0.6 53.5 %copy-start = (bf16[512,512]{1,0:T(8,128)(2,1)S(1)}, bf16[512,512]{1,0:T(8,128)(2,1)}, u32[]{:S(2)}) copy-start(bf16[512,512]{1,0:T(8,128)(2,1)} %param.19) | copy-start | bytes 1572868
  2.3 17.8 %copy-start.4 = (bf16[1024,512]{1,0:T(8,128)(2,1)S(1)}, bf16[1024,512]{1,0:T(8,128)(2,1)}, u32[]{:S(2)}) copy-start(bf16[1024,512]{1,0:T(8,128)(2,1)} %param.13) | copy-start | bytes 3145732
  2.3 17.8 %copy-start.17 = (bf16[1536,512]{1,0:T(8,128)(2,1)S(1)}, bf16[1536,512]{1,0:T(8,128)(2,1)}, u32[]{:S(2)}) copy-start(bf16[1536,512]{1,0:T(8,128)(2,1)} %param.18) | copy-start | bytes 4718596
  3.6 20.7 %collective-permute-start = (bf16[128,512]{1,0:T(8,128)(2,1)S(1)}, bf16[128,512]{1,0:T(8,128)(2,1)S(1)}, u32[]{:S(2)}, u32[]{:S(2)}) collective-permute-start(bf16[128,512]{1,0:T(8,128)(2,1)S(1)} %bitcast.313), channel_id=1, source_target_pairs={{0,16},{16,32},{32,48},{48,64},{64,80},{80,96},{96,112},{1,17},{17... | collective-permute-start | bytes 393224 | tf_op jit(solution)/shard_map/ppermute | solution.py:12
  6.8 24.5 %collective-permute-start.1 = (bf16[128,512]{1,0:T(8,128)(2,1)S(1)}, bf16[128,512]{1,0:T(8,128)(2,1)S(1)}, u32[]{:S(2)}, u32[]{:S(2)}) collective-permute-start(bf16[128,512]{1,0:T(8,128)(2,1)S(1)} %bitcast.305), channel_id=1, source_target_pairs={{16,0},{32,16},{48,32},{64,48},{80,64},{96,80},{112,96},{17,1},{33... | collective-permute-start | bytes 393224 | tf_op jit(solution)/shard_map/ppermute | solution.py:12
  11.6 20.6 %collective-permute-start.2 = (bf16[128,512]{1,0:T(8,128)(2,1)}, bf16[128,512]{1,0:T(8,128)(2,1)}, u32[]{:S(2)}, u32[]{:S(2)}) collective-permute-start(bf16[128,512]{1,0:T(8,128)(2,1)} %bitcast.275), channel_id=1, source_target_pairs={{0,1},{1,2},{2,3},{3,4},{4,5},{5,6},{6,7},{7,8},{8,9},{9,10},{10,1... | collective-permute-start | bytes 393224 | tf_op jit(solution)/shard_map/ppermute | solution.py:12
  14.2 7.9 %copy-start.2 = (bf16[512,512]{1,0:T(8,128)(2,1)S(1)}, bf16[512,512]{1,0:T(8,128)(2,1)}, u32[]{:S(2)}) copy-start(bf16[512,512]{1,0:T(8,128)(2,1)} %param.12) | copy-start | bytes 1572868
  14.2 19.8 %collective-permute-start.3 = (bf16[128,512]{1,0:T(8,128)(2,1)}, bf16[128,512]{1,0:T(8,128)(2,1)}, u32[]{:S(2)}, u32[]{:S(2)}) collective-permute-start(bf16[128,512]{1,0:T(8,128)(2,1)} %bitcast.274), channel_id=1, source_target_pairs={{1,0},{2,1},{3,2},{4,3},{5,4},{6,5},{7,6},{8,7},{9,8},{10,9},{11,1... | collective-permute-start | bytes 393224 | tf_op jit(solution)/shard_map/ppermute | solution.py:12
  16.3 19.5 %collective-permute-start.4 = (bf16[128,512]{1,0:T(8,128)(2,1)}, bf16[128,512]{1,0:T(8,128)(2,1)}, u32[]{:S(2)}, u32[]{:S(2)}) collective-permute-start(bf16[128,512]{1,0:T(8,128)(2,1)} %bitcast.273), channel_id=1, source_target_pairs={{0,128},{1,129},{2,130},{3,131},{4,132},{5,133},{6,134},{7,135},{8... | collective-permute-start | bytes 393224 | tf_op jit(solution)/shard_map/ppermute | solution.py:12
  24.2 13.4 %collective-permute-start.5 = (bf16[128,512]{1,0:T(8,128)(2,1)}, bf16[128,512]{1,0:T(8,128)(2,1)}, u32[]{:S(2)}, u32[]{:S(2)}) collective-permute-start(bf16[128,512]{1,0:T(8,128)(2,1)} %bitcast.272), channel_id=1, source_target_pairs={{128,0},{129,1},{130,2},{131,3},{132,4},{133,5},{134,6},{135,7},{1... | collective-permute-start | bytes 393224 | tf_op jit(solution)/shard_map/ppermute | solution.py:12
  39.4 13.1 %copy-start.27 = (bf16[4,2,128,128]{3,2,1,0:T(8,128)(2,1)S(1)}, bf16[4,2,128,128]{3,2,1,0:T(8,128)(2,1)}, u32[]{:S(2)}) copy-start(bf16[4,2,128,128]{3,2,1,0:T(8,128)(2,1)} %param.14) | copy-start | bytes 786436
  95.4 71.3 %collective-permute-start.20 = (f32[2,2,2,2,2,2,2,1024]{7,2,4,6,5,0,3,1:T(2,128)}, f32[2,2,2,2,2,2,2,1024]{7,2,4,6,5,0,3,1:T(2,128)}, u32[]{:S(2)}, u32[]{:S(2)}) collective-permute-start(f32[2,2,2,2,2,2,2,1024]{7,2,4,6,5,0,3,1:T(2,128)} %bitcast.264), channel_id=1, source_target_pairs={{0,1},{1,0},{2,3},{3,2},{4,5},{5,4},{6,7},{7,6},{8,9},{9,8},{10,11... | collective-permute-start | bytes 1572872 | tf_op jit(solution)/shard_map/ppermute | solution.py:32
  97.8 71.9 %collective-permute-start.36 = (f32[2,2,2,2,2,2,2,1024]{7,2,4,6,5,0,3,1:T(2,128)}, f32[2,2,2,2,2,2,2,1024]{7,2,4,6,5,0,3,1:T(2,128)}, u32[]{:S(2)}, u32[]{:S(2)}) collective-permute-start(f32[2,2,2,2,2,2,2,1024]{7,2,4,6,5,0,3,1:T(2,128)} %bitcast.262), channel_id=1, source_target_pairs={{0,1},{1,0},{2,3},{3,2},{4,5},{5,4},{6,7},{7,6},{8,9},{9,8},{10,11... | collective-permute-start | bytes 1572872 | tf_op jit(solution)/shard_map/ppermute | solution.py:32
  108.7 8.0 %copy-start.3 = (bf16[10,128,512]{2,0,1:T(8,128)(2,1)S(1)}, bf16[10,128,512]{2,0,1:T(8,128)(2,1)}, u32[]{:S(2)}) copy-start(bf16[10,128,512]{2,0,1:T(8,128)(2,1)} %convolution_convert_fusion) | copy-start | bytes 3932164
  116.7 10.6 %copy-start.7 = (f32[2,2,2,2,2,2,2,2,2048]{8,7,6,5,4,3,2,1,0:T(2,128)S(1)}, f32[2,2,2,2,2,2,2,2,2048]{8,7,6,5,4,3,2,1,0:T(2,128)}, u32[]{:S(2)}) copy-start(f32[2,2,2,2,2,2,2,2,2048]{8,7,6,5,4,3,2,1,0:T(2,128)} %reshape.122) | copy-start | bytes 6291460
  118.0 14.2 %collective-permute-start.6 = (bf16[128,512]{1,0:T(8,128)(2,1)S(1)}, bf16[128,512]{1,0:T(8,128)(2,1)S(1)}, u32[]{:S(2)}, u32[]{:S(2)}) collective-permute-start(bf16[128,512]{1,0:T(8,128)(2,1)S(1)} %bitcast.314), channel_id=1, source_target_pairs={{0,16},{16,32},{32,48},{48,64},{64,80},{80,96},{96,112},{1,17},{17... | collective-permute-start | bytes 393224 | tf_op jit(solution)/shard_map/ppermute | solution.py:12
  122.4 11.1 %collective-permute-start.7 = (bf16[128,512]{1,0:T(8,128)(2,1)S(1)}, bf16[128,512]{1,0:T(8,128)(2,1)S(1)}, u32[]{:S(2)}, u32[]{:S(2)}) collective-permute-start(bf16[128,512]{1,0:T(8,128)(2,1)S(1)} %bitcast.312), channel_id=1, source_target_pairs={{16,0},{32,16},{48,32},{64,48},{80,64},{96,80},{112,96},{17,1},{33... | collective-permute-start | bytes 393224 | tf_op jit(solution)/shard_map/ppermute | solution.py:12
  125.3 15.2 %copy-start.25 = (bf16[4,128,512]{2,1,0:T(8,128)(2,1)S(1)}, bf16[4,128,512]{2,1,0:T(8,128)(2,1)}, u32[]{:S(2)}) copy-start(bf16[4,128,512]{2,1,0:T(8,128)(2,1)} %copy-done.24) | copy-start | bytes 1572868
  125.4 13.7 %collective-permute-start.8 = (bf16[128,512]{1,0:T(8,128)(2,1)S(1)}, bf16[128,512]{1,0:T(8,128)(2,1)S(1)}, u32[]{:S(2)}, u32[]{:S(2)}) collective-permute-start(bf16[128,512]{1,0:T(8,128)(2,1)S(1)} %bitcast.311), channel_id=1, source_target_pairs={{0,1},{1,2},{2,3},{3,4},{4,5},{5,6},{6,7},{7,8},{8,9},{9,10},{10,1... | collective-permute-start | bytes 393224 | tf_op jit(solution)/shard_map/ppermute | solution.py:12
  130.8 12.1 %copy-start.29 = (bf16[512,512]{1,0:T(8,128)(2,1)S(1)}, bf16[512,512]{1,0:T(8,128)(2,1)}, u32[]{:S(2)}) copy-start(bf16[512,512]{1,0:T(8,128)(2,1)} %fusion.19) | copy-start | bytes 1572868
  130.9 13.2 %copy-start.23 = (bf16[512,512]{0,1:T(8,128)(2,1)S(1)}, bf16[512,512]{0,1:T(8,128)(2,1)}, u32[]{:S(2)}) copy-start(bf16[512,512]{0,1:T(8,128)(2,1)} %get-tuple-element.80) | copy-start | bytes 1572868
  132.2 19.8 %collective-permute-start.9 = (bf16[128,512]{1,0:T(8,128)(2,1)}, bf16[128,512]{1,0:T(8,128)(2,1)}, u32[]{:S(2)}, u32[]{:S(2)}) collective-permute-start(bf16[128,512]{1,0:T(8,128)(2,1)} %bitcast.268), channel_id=1, source_target_pairs={{1,0},{2,1},{3,2},{4,3},{5,4},{6,5},{7,6},{8,7},{9,8},{10,9},{11,1... | collective-permute-start | bytes 393224 | tf_op jit(solution)/shard_map/ppermute | solution.py:12
  133.5 23.6 %collective-permute-start.10 = (bf16[128,512]{1,0:T(8,128)(2,1)}, bf16[128,512]{1,0:T(8,128)(2,1)}, u32[]{:S(2)}, u32[]{:S(2)}) collective-permute-start(bf16[128,512]{1,0:T(8,128)(2,1)} %bitcast.267), channel_id=1, source_target_pairs={{0,128},{1,129},{2,130},{3,131},{4,132},{5,133},{6,134},{7,135},{8... | collective-permute-start | bytes 393224 | tf_op jit(solution)/shard_map/ppermute | solution.py:12
  139.1 6.0 %copy-start.32 = (bf16[128,512]{1,0:T(8,128)(2,1)}, bf16[128,512]{1,0:T(8,128)(2,1)S(1)}, u32[]{:S(2)}) copy-start(bf16[128,512]{1,0:T(8,128)(2,1)S(1)} %collective-permute-done.8) | copy-start | bytes 393220
  139.1 19.8 %collective-permute-start.11 = (bf16[128,512]{1,0:T(8,128)(2,1)S(1)}, bf16[128,512]{1,0:T(8,128)(2,1)}, u32[]{:S(2)}, u32[]{:S(2)}) collective-permute-start(bf16[128,512]{1,0:T(8,128)(2,1)S(1)} %bitcast.307), channel_id=1, source_target_pairs={{128,0},{129,1},{130,2},{131,3},{132,4},{133,5},{134,6},{135,7},{1... | collective-permute-start | bytes 393224 | tf_op jit(solution)/shard_map/ppermute | solution.py:12
  151.1 15.5 %copy-start.22 = (f32[2,2,2,2,2,2,2,1,1024]{8,7,6,5,4,3,2,1,0:T(1,128)S(1)}, f32[2,2,2,2,2,2,2,1,1024]{8,7,6,5,4,3,2,1,0:T(1,128)}, u32[]{:S(2)}) copy-start(f32[2,2,2,2,2,2,2,1,1024]{8,7,6,5,4,3,2,1,0:T(1,128)} %get-tuple-element.124) | copy-start | bytes 1572868
  152.1 58.6 %collective-permute-start.28 = (f32[2,2,2,2,2,2,2,2048]{7,0,4,5,3,1,6,2:T(2,128)}, f32[2,2,2,2,2,2,2,2048]{7,0,4,5,3,1,6,2:T(2,128)}, u32[]{:S(2)}, u32[]{:S(2)}) collective-permute-start(f32[2,2,2,2,2,2,2,2048]{7,0,4,5,3,1,6,2:T(2,128)} %bitcast.261), channel_id=1, source_target_pairs={{0,1},{1,0},{2,3},{3,2},{4,5},{5,4},{6,7},{7,6},{8,9},{9,8},{10,11... | collective-permute-start | bytes 3145736 | tf_op jit(solution)/shard_map/ppermute | solution.py:32
  157.1 68.9 %collective-permute-start.12 = (f32[2,2,2,2,2,2,2,3072]{7,1,3,6,4,2,5,0:T(2,128)}, f32[2,2,2,2,2,2,2,3072]{7,1,3,6,4,2,5,0:T(2,128)}, u32[]{:S(2)}, u32[]{:S(2)}) collective-permute-start(f32[2,2,2,2,2,2,2,3072]{7,1,3,6,4,2,5,0:T(2,128)} %bitcast.260), channel_id=1, source_target_pairs={{0,1},{1,0},{2,3},{3,2},{4,5},{5,4},{6,7},{7,6},{8,9},{9,8},{10,11... | collective-permute-start | bytes 4718600 | tf_op jit(solution)/shard_map/ppermute | solution.py:32
  160.7 9.0 %copy-start.21 = (f32[2,2,2,2,2,2,2,1,1024]{8,7,6,5,4,3,2,1,0:T(1,128)S(1)}, f32[2,2,2,2,2,2,2,1,1024]{8,7,6,5,4,3,2,1,0:T(1,128)}, u32[]{:S(2)}) copy-start(f32[2,2,2,2,2,2,2,1,1024]{8,7,6,5,4,3,2,1,0:T(1,128)} %get-tuple-element.81) | copy-start | bytes 1572868
  168.1 9.3 %collective-permute-start.21 = (f32[2,2,2,2,2,2,1024]{6,1,3,5,4,2,0:T(2,128)S(1)}, f32[2,2,2,2,2,2,1024]{6,1,3,5,4,2,0:T(2,128)S(1)}, u32[]{:S(2)}, u32[]{:S(2)}) collective-permute-start(f32[2,2,2,2,2,2,1024]{6,1,3,5,4,2,0:T(2,128)S(1)} %dynamic-slice_bitcast_fusion.7), channel_id=1, source_target_pairs={{0,32},{16,48},{32,0},{48,16},{64,96},{80,112},{96,64},{112,80},{1... | collective-permute-start | bytes 786440 | tf_op jit(solution)/shard_map/ppermute | solution.py:32
  171.2 11.4 %collective-permute-start.37 = (f32[2,2,2,2,2,2,1024]{6,1,3,5,4,2,0:T(2,128)S(1)}, f32[2,2,2,2,2,2,1024]{6,1,3,5,4,2,0:T(2,128)S(1)}, u32[]{:S(2)}, u32[]{:S(2)}) collective-permute-start(f32[2,2,2,2,2,2,1024]{6,1,3,5,4,2,0:T(2,128)S(1)} %dynamic-slice_bitcast_fusion.5), channel_id=1, source_target_pairs={{0,32},{16,48},{32,0},{48,16},{64,96},{80,112},{96,64},{112,80},{1... | collective-permute-start | bytes 786440 | tf_op jit(solution)/shard_map/ppermute | solution.py:32
  177.5 33.1 %copy-start.10 = (f32[2,2,2,2,2,2,2,1,2048]{8,7,6,5,4,3,2,1,0:T(1,128)S(1)}, f32[2,2,2,2,2,2,2,1,2048]{8,7,6,5,4,3,2,1,0:T(1,128)}, u32[]{:S(2)}) copy-start(f32[2,2,2,2,2,2,2,1,2048]{8,7,6,5,4,3,2,1,0:T(1,128)} %get-tuple-element.71) | copy-start | bytes 3145732
  177.6 8.2 %collective-permute-start.22 = (f32[2,2,2,2,2,1024]{5,0,2,4,3,1:T(2,128)S(1)}, f32[2,2,2,2,2,1024]{5,0,2,4,3,1:T(2,128)S(1)}, u32[]{:S(2)}, u32[]{:S(2)}) collective-permute-start(f32[2,2,2,2,2,1024]{5,0,2,4,3,1:T(2,128)S(1)} %dynamic-slice_bitcast_fusion.11), channel_id=1, source_target_pairs={{0,128},{128,0},{1,129},{129,1},{2,130},{130,2},{3,131},{131,3},{4... | collective-permute-start | bytes 393224 | tf_op jit(solution)/shard_map/ppermute | solution.py:32
  182.7 6.4 %collective-permute-start.38 = (f32[2,2,2,2,2,1024]{5,0,2,4,3,1:T(2,128)S(1)}, f32[2,2,2,2,2,1024]{5,0,2,4,3,1:T(2,128)S(1)}, u32[]{:S(2)}, u32[]{:S(2)}) collective-permute-start(f32[2,2,2,2,2,1024]{5,0,2,4,3,1:T(2,128)S(1)} %dynamic-slice_bitcast_fusion.9), channel_id=1, source_target_pairs={{0,128},{128,0},{1,129},{129,1},{2,130},{130,2},{3,131},{131,3},{4... | collective-permute-start | bytes 393224 | tf_op jit(solution)/shard_map/ppermute | solution.py:32
  186.0 5.2 %collective-permute-start.23 = (f32[2,2,2,2,1024]{4,1,3,2,0:T(2,128)S(1)}, f32[2,2,2,2,1024]{4,1,3,2,0:T(2,128)S(1)}, u32[]{:S(2)}, u32[]{:S(2)}) collective-permute-start(f32[2,2,2,2,1024]{4,1,3,2,0:T(2,128)S(1)} %bitcast.316), channel_id=1, source_target_pairs={{0,2},{1,3},{2,0},{3,1},{4,6},{5,7},{6,4},{7,5},{8,10},{9,11},{10,... | collective-permute-start | bytes 196616 | tf_op jit(solution)/shard_map/ppermute | solution.py:32
  189.3 5.1 %collective-permute-start.39 = (f32[2,2,2,2,1024]{4,1,3,2,0:T(2,128)S(1)}, f32[2,2,2,2,1024]{4,1,3,2,0:T(2,128)S(1)}, u32[]{:S(2)}, u32[]{:S(2)}) collective-permute-start(f32[2,2,2,2,1024]{4,1,3,2,0:T(2,128)S(1)} %bitcast.317), channel_id=1, source_target_pairs={{0,2},{1,3},{2,0},{3,1},{4,6},{5,7},{6,4},{7,5},{8,10},{9,11},{10,... | collective-permute-start | bytes 196616 | tf_op jit(solution)/shard_map/ppermute | solution.py:32
  191.3 5.8 %collective-permute-start.24 = (f32[2,2,2,1024]{3,0,2,1:T(2,128)S(1)}, f32[2,2,2,1024]{3,0,2,1:T(2,128)S(1)}, u32[]{:S(2)}, u32[]{:S(2)}) collective-permute-start(f32[2,2,2,1024]{3,0,2,1:T(2,128)S(1)} %dynamic-slice_bitcast_fusion.15), channel_id=1, source_target_pairs={{0,64},{16,80},{32,96},{48,112},{64,0},{80,16},{96,32},{112,48},{1... | collective-permute-start | bytes 98312 | tf_op jit(solution)/shard_map/ppermute | solution.py:32
  194.5 8.3 %collective-permute-start.40 = (f32[2,2,2,1024]{3,0,2,1:T(2,128)S(1)}, f32[2,2,2,1024]{3,0,2,1:T(2,128)S(1)}, u32[]{:S(2)}, u32[]{:S(2)}) collective-permute-start(f32[2,2,2,1024]{3,0,2,1:T(2,128)S(1)} %dynamic-slice_bitcast_fusion.14), channel_id=1, source_target_pairs={{0,64},{16,80},{32,96},{48,112},{64,0},{80,16},{96,32},{112,48},{1... | collective-permute-start | bytes 98312 | tf_op jit(solution)/shard_map/ppermute | solution.py:32
  197.2 9.2 %collective-permute-start.25 = (f32[2,2,1024]{2,1,0:T(2,128)S(1)}, f32[2,2,1024]{2,1,0:T(2,128)S(1)}, u32[]{:S(2)}, u32[]{:S(2)}) collective-permute-start(f32[2,2,1024]{2,1,0:T(2,128)S(1)} %bitcast.325), channel_id=1, source_target_pairs={{0,4},{1,5},{2,6},{3,7},{4,0},{5,1},{6,2},{7,3},{8,12},{9,13},{10,... | collective-permute-start | bytes 49160 | tf_op jit(solution)/shard_map/ppermute | solution.py:32
  202.9 6.1 %collective-permute-start.41 = (f32[2,2,1024]{2,1,0:T(2,128)S(1)}, f32[2,2,1024]{2,1,0:T(2,128)S(1)}, u32[]{:S(2)}, u32[]{:S(2)}) collective-permute-start(f32[2,2,1024]{2,1,0:T(2,128)S(1)} %bitcast.327), channel_id=1, source_target_pairs={{0,4},{1,5},{2,6},{3,7},{4,0},{5,1},{6,2},{7,3},{8,12},{9,13},{10,... | collective-permute-start | bytes 49160 | tf_op jit(solution)/shard_map/ppermute | solution.py:32
  206.4 9.5 %collective-permute-start.26 = (f32[2,1024]{1,0:T(2,128)S(1)}, f32[2,1024]{1,0:T(2,128)S(1)}, u32[]{:S(2)}, u32[]{:S(2)}) collective-permute-start(f32[2,1024]{1,0:T(2,128)S(1)} %fusion.52), channel_id=1, source_target_pairs={{0,16},{16,0},{32,48},{48,32},{64,80},{80,64},{96,112},{112,96},{1... | collective-permute-start | bytes 24584 | tf_op jit(solution)/shard_map/ppermute | solution.py:32
  209.0 12.2 %collective-permute-start.42 = (f32[2,1024]{1,0:T(2,128)S(1)}, f32[2,1024]{1,0:T(2,128)S(1)}, u32[]{:S(2)}, u32[]{:S(2)}) collective-permute-start(f32[2,1024]{1,0:T(2,128)S(1)} %fusion.55), channel_id=1, source_target_pairs={{0,16},{16,0},{32,48},{48,32},{64,80},{80,64},{96,112},{112,96},{1... | collective-permute-start | bytes 24584 | tf_op jit(solution)/shard_map/ppermute | solution.py:32
  213.8 12.1 %copy-start.9 = (f32[2,2,2,2,2,2,2,1,3072]{8,7,6,5,4,3,2,1,0:T(1,128)S(1)}, f32[2,2,2,2,2,2,2,1,3072]{8,7,6,5,4,3,2,1,0:T(1,128)}, u32[]{:S(2)}) copy-start(f32[2,2,2,2,2,2,2,1,3072]{8,7,6,5,4,3,2,1,0:T(1,128)} %get-tuple-element.69) | copy-start | bytes 4718596
  214.1 10.3 %collective-permute-start.29 = (f32[2,2,2,2,2,2,2048]{6,3,4,2,0,5,1:T(2,128)S(1)}, f32[2,2,2,2,2,2,2048]{6,3,4,2,0,5,1:T(2,128)S(1)}, u32[]{:S(2)}, u32[]{:S(2)}) collective-permute-start(f32[2,2,2,2,2,2,2048]{6,3,4,2,0,5,1:T(2,128)S(1)} %bitcast.302), channel_id=1, source_target_pairs={{0,2},{1,3},{2,0},{3,1},{4,6},{5,7},{6,4},{7,5},{8,10},{9,11},{10,... | collective-permute-start | bytes 1572872 | tf_op jit(solution)/shard_map/ppermute | solution.py:32
  216.0 74.8 %collective-permute-start.27 = (f32[1024]{0:T(1024)S(1)}, f32[1024]{0:T(1024)S(1)}, u32[]{:S(2)}, u32[]{:S(2)}) collective-permute-start(f32[1024]{0:T(1024)S(1)} %bitcast.330), channel_id=1, source_target_pairs={{0,8},{1,9},{2,10},{3,11},{4,12},{5,13},{6,14},{7,15},{8,0},{9,1},... | collective-permute-start | bytes 12296 | tf_op jit(solution)/shard_map/ppermute | solution.py:32
  224.8 6.5 %collective-permute-start.30 = (f32[2,2,2,2,2,2048]{5,2,3,1,4,0:T(2,128)S(1)}, f32[2,2,2,2,2,2048]{5,2,3,1,4,0:T(2,128)S(1)}, u32[]{:S(2)}, u32[]{:S(2)}) collective-permute-start(f32[2,2,2,2,2,2048]{5,2,3,1,4,0:T(2,128)S(1)} %dynamic-slice_bitcast_fusion.6), channel_id=1, source_target_pairs={{0,32},{16,48},{32,0},{48,16},{64,96},{80,112},{96,64},{112,80},{1... | collective-permute-start | bytes 786440 | tf_op jit(solution)/shard_map/ppermute | solution.py:32
  231.5 8.2 %collective-permute-start.31 = (f32[2,2,2,2,2048]{4,1,2,0,3:T(2,128)S(1)}, f32[2,2,2,2,2048]{4,1,2,0,3:T(2,128)S(1)}, u32[]{:S(2)}, u32[]{:S(2)}) collective-permute-start(f32[2,2,2,2,2048]{4,1,2,0,3:T(2,128)S(1)} %dynamic-slice_bitcast_fusion.10), channel_id=1, source_target_pairs={{0,128},{128,0},{1,129},{129,1},{2,130},{130,2},{3,131},{131,3},{4... | collective-permute-start | bytes 393224 | tf_op jit(solution)/shard_map/ppermute | solution.py:32
  234.0 15.6 %collective-permute-start.13 = (f32[2,2,2,2,2,2,3072]{6,0,2,5,3,1,4:T(2,128)S(1)}, f32[2,2,2,2,2,2,3072]{6,0,2,5,3,1,4:T(2,128)S(1)}, u32[]{:S(2)}, u32[]{:S(2)}) collective-permute-start(f32[2,2,2,2,2,2,3072]{6,0,2,5,3,1,4:T(2,128)S(1)} %dynamic-slice_bitcast_fusion.2), channel_id=1, source_target_pairs={{0,128},{128,0},{1,129},{129,1},{2,130},{130,2},{3,131},{131,3},{4... | collective-permute-start | bytes 2359304 | tf_op jit(solution)/shard_map/ppermute | solution.py:32
  234.1 57.3 %collective-permute-start.43 = (f32[1024]{0:T(1024)S(1)}, f32[1024]{0:T(1024)S(1)}, u32[]{:S(2)}, u32[]{:S(2)}) collective-permute-start(f32[1024]{0:T(1024)S(1)} %bitcast.331), channel_id=1, source_target_pairs={{0,8},{1,9},{2,10},{3,11},{4,12},{5,13},{6,14},{7,15},{8,0},{9,1},... | collective-permute-start | bytes 12296 | tf_op jit(solution)/shard_map/ppermute | solution.py:32
  239.8 12.4 %collective-permute-start.32 = (f32[2,2,2,2048]{3,0,1,2:T(2,128)S(1)}, f32[2,2,2,2048]{3,0,1,2:T(2,128)S(1)}, u32[]{:S(2)}, u32[]{:S(2)}) collective-permute-start(f32[2,2,2,2048]{3,0,1,2:T(2,128)S(1)} %dynamic-slice_bitcast_fusion.12), channel_id=1, source_target_pairs={{0,16},{16,0},{32,48},{48,32},{64,80},{80,64},{96,112},{112,96},{1... | collective-permute-start | bytes 196616 | tf_op jit(solution)/shard_map/ppermute | solution.py:32
  251.2 37.1 %copy-start.11 = (f32[4,128,512]{2,1,0:T(8,128)S(1)}, f32[4,128,512]{2,1,0:T(8,128)}, u32[]{:S(2)}) copy-start(f32[4,128,512]{2,1,0:T(8,128)} %convert.6) | copy-start | bytes 3145732
  251.2 37.1 %copy-start.12 = (bf16[6,128,512]{2,0,1:T(8,128)(2,1)S(1)}, bf16[6,128,512]{2,0,1:T(8,128)(2,1)}, u32[]{:S(2)}) copy-start(bf16[6,128,512]{2,0,1:T(8,128)(2,1)} %stack.51) | copy-start | bytes 2359300
  251.2 37.1 %copy-start.28 = (bf16[512,512]{1,0:T(8,128)(2,1)S(1)}, bf16[512,512]{1,0:T(8,128)(2,1)}, u32[]{:S(2)}) copy-start(bf16[512,512]{1,0:T(8,128)(2,1)} %convolution_convert_fusion.12) | copy-start | bytes 1572868
  251.2 37.1 %copy-start.34 = (s32[1,6]{1,0:T(1,128)S(1)}, s32[1,6]{1,0:T(1,128)}, u32[]{:S(2)}) copy-start(s32[1,6]{1,0:T(1,128)} %param.17) | copy-start | bytes 76
  251.2 8.2 %collective-permute-start.14 = (f32[2,2,2,2,2,3072]{5,1,4,2,0,3:T(2,128)S(1)}, f32[2,2,2,2,2,3072]{5,1,4,2,0,3:T(2,128)S(1)}, u32[]{:S(2)}, u32[]{:S(2)}) collective-permute-start(f32[2,2,2,2,2,3072]{5,1,4,2,0,3:T(2,128)S(1)} %bitcast.303), channel_id=1, source_target_pairs={{0,2},{1,3},{2,0},{3,1},{4,6},{5,7},{6,4},{7,5},{8,10},{9,11},{10,... | collective-permute-start | bytes 1179656 | tf_op jit(solution)/shard_map/ppermute | solution.py:32
  252.3 7.8 %collective-permute-start.33 = (f32[2,2,2048]{2,0,1:T(2,128)S(1)}, f32[2,2,2048]{2,0,1:T(2,128)S(1)}, u32[]{:S(2)}, u32[]{:S(2)}) collective-permute-start(f32[2,2,2048]{2,0,1:T(2,128)S(1)} %bitcast.321), channel_id=1, source_target_pairs={{0,4},{1,5},{2,6},{3,7},{4,0},{5,1},{6,2},{7,3},{8,12},{9,13},{10,... | collective-permute-start | bytes 98312 | tf_op jit(solution)/shard_map/ppermute | solution.py:32
  259.7 5.8 %collective-permute-start.15 = (f32[2,2,2,2,3072]{4,0,3,1,2:T(2,128)S(1)}, f32[2,2,2,2,3072]{4,0,3,1,2:T(2,128)S(1)}, u32[]{:S(2)}, u32[]{:S(2)}) collective-permute-start(f32[2,2,2,2,3072]{4,0,3,1,2:T(2,128)S(1)} %dynamic-slice_bitcast_fusion.8), channel_id=1, source_target_pairs={{0,32},{16,48},{32,0},{48,16},{64,96},{80,112},{96,64},{112,80},{1... | collective-permute-start | bytes 589832 | tf_op jit(solution)/shard_map/ppermute | solution.py:32
  265.8 6.6 %collective-permute-start.16 = (f32[2,2,2,3072]{3,2,0,1:T(2,128)S(1)}, f32[2,2,2,3072]{3,2,0,1:T(2,128)S(1)}, u32[]{:S(2)}, u32[]{:S(2)}) collective-permute-start(f32[2,2,2,3072]{3,2,0,1:T(2,128)S(1)} %bitcast.315), channel_id=1, source_target_pairs={{0,4},{1,5},{2,6},{3,7},{4,0},{5,1},{6,2},{7,3},{8,12},{9,13},{10,... | collective-permute-start | bytes 294920 | tf_op jit(solution)/shard_map/ppermute | solution.py:32
  268.8 7.7 %collective-permute-start.34 = (f32[2,2048]{1,0:T(2,128)S(1)}, f32[2,2048]{1,0:T(2,128)S(1)}, u32[]{:S(2)}, u32[]{:S(2)}) collective-permute-start(f32[2,2048]{1,0:T(2,128)S(1)} %bitcast.326), channel_id=1, source_target_pairs={{0,8},{1,9},{2,10},{3,11},{4,12},{5,13},{6,14},{7,15},{8,0},{9,1},... | collective-permute-start | bytes 49160 | tf_op jit(solution)/shard_map/ppermute | solution.py:32
  272.5 5.7 %collective-permute-start.17 = (f32[2,2,3072]{2,1,0:T(2,128)S(1)}, f32[2,2,3072]{2,1,0:T(2,128)S(1)}, u32[]{:S(2)}, u32[]{:S(2)}) collective-permute-start(f32[2,2,3072]{2,1,0:T(2,128)S(1)} %dynamic-slice_bitcast_fusion.13), channel_id=1, source_target_pairs={{0,16},{16,0},{32,48},{48,32},{64,80},{80,64},{96,112},{112,96},{1... | collective-permute-start | bytes 147464 | tf_op jit(solution)/shard_map/ppermute | solution.py:32
  278.3 5.4 %collective-permute-start.18 = (f32[2,3072]{1,0:T(2,128)S(1)}, f32[2,3072]{1,0:T(2,128)S(1)}, u32[]{:S(2)}, u32[]{:S(2)}) collective-permute-start(f32[2,3072]{1,0:T(2,128)S(1)} %dynamic-slice_bitcast_fusion.16), channel_id=1, source_target_pairs={{0,64},{16,80},{32,96},{48,112},{64,0},{80,16},{96,32},{112,48},{1... | collective-permute-start | bytes 73736 | tf_op jit(solution)/shard_map/ppermute | solution.py:32
  280.3 11.6 %collective-permute-start.35 = (f32[2048]{0:T(1024)S(1)}, f32[2048]{0:T(1024)S(1)}, u32[]{:S(2)}, u32[]{:S(2)}) collective-permute-start(f32[2048]{0:T(1024)S(1)} %bitcast.329), channel_id=1, source_target_pairs={{0,64},{16,80},{32,96},{48,112},{64,0},{80,16},{96,32},{112,48},{1... | collective-permute-start | bytes 24584 | tf_op jit(solution)/shard_map/ppermute | solution.py:32
  283.8 8.8 %collective-permute-start.19 = (f32[3072]{0:T(1024)S(1)}, f32[3072]{0:T(1024)S(1)}, u32[]{:S(2)}, u32[]{:S(2)}) collective-permute-start(f32[3072]{0:T(1024)S(1)} %bitcast.328), channel_id=1, source_target_pairs={{0,8},{1,9},{2,10},{3,11},{4,12},{5,13},{6,14},{7,15},{8,0},{9,1},... | collective-permute-start | bytes 36872 | tf_op jit(solution)/shard_map/ppermute | solution.py:32
  288.3 4.9 %copy-start.1 = (bf16[512,512]{1,0:T(8,128)(2,1)S(1)}, bf16[512,512]{1,0:T(8,128)(2,1)}, u32[]{:S(2)}) copy-start(bf16[512,512]{1,0:T(8,128)(2,1)} %param.19) | copy-start | bytes 1572868
  (18 other events, 51.0 us)

commit v2 on v1

--- a/solution.py
+++ b/solution.py
@@ -13,16 +13,12 @@
 
 
 INDEX_BITS = (("segment", 0), ("gx", 2), ("gx", 1), ("gx", 0), ("gy", 3), ("gy", 2), ("gy", 1), ("gy", 0))
-EDGE_IN_ORDER = (7, 0, 6, 2, 5, 3, 1, 4)
-EDGE_OUT_ORDER = (7, 2, 0, 6, 1, 5, 3, 4)
-NODE_IN_ORDER = (7, 6, 2, 0, 3, 5, 4, 1)
-NODE_OUT_ORDER = (7, 2, 0, 6, 1, 5, 3, 4)
-
-
-def halving_scatter(flat, order):
-    devices = 1 << len(INDEX_BITS)
-    share = flat.shape[0] // devices
-    parts = flat.reshape((2,) * len(INDEX_BITS) + (share,)).transpose(tuple(order) + (len(INDEX_BITS),))
+EDGE_ORDER = (7, 0, 6, 2, 5, 3, 1, 4)
+NODE_ORDER = (7, 6, 2, 0, 3, 5, 4, 1)
+
+def halving_scatter(rows, order):
+    bits = len(INDEX_BITS)
+    parts = rows.reshape((2,) * bits + rows.shape[1:]).transpose(tuple(order) + (bits,))
     for position in order:
         axis, bit = INDEX_BITS[position]
         side = (lax.axis_index(axis) >> bit) & 1
@@ -168,11 +164,20 @@
         "jn,jbd->nbd", choose, returned, preferred_element_type=jnp.float32
     )
     edge_terms = (grad_ei.astype(jnp.float32).reshape(-1), grad_eo.astype(jnp.float32).reshape(-1))
+    devices = 1 << len(INDEX_BITS)
+    edge_share = halving_scatter(
+        jnp.concatenate([term.reshape(devices, -1) for term in edge_terms], axis=1), EDGE_ORDER
+    )
+    node_share = halving_scatter(
+        jnp.concatenate([term.reshape(devices, -1) for term in node_terms], axis=1), NODE_ORDER
+    )
+    edge_cut = edge_terms[0].shape[0] // devices
+    node_cut = node_terms[0].shape[0] // devices
     shares = (
-        halving_scatter(edge_terms[0], EDGE_IN_ORDER),
-        halving_scatter(edge_terms[1], EDGE_OUT_ORDER),
-        halving_scatter(node_terms[0], NODE_IN_ORDER),
-        halving_scatter(node_terms[1], NODE_OUT_ORDER),
+        edge_share[:edge_cut],
+        edge_share[edge_cut:],
+        node_share[:node_cut],
+        node_share[node_cut:],
     )
     return (
         outputs[0],

time: 299 us -> 271 us (0.906)
  starting transfers between devices: 105 us -> 67.5 us
  waiting for transfers between devices: 42.4 us -> 63.5 us
  local copies, waits for them, and re-layouts: 87.7 us -> 73.5 us
  other arithmetic: 21.8 us -> 26.4 us
    ppermute x32 -> x16, starting transfers between devices: 71.2 us -> 33.5 us  [halving_scatter(): parts = keep + lax.ppermute(send, axis, route)]
    another operation x7 -> x2, local copies, waits for them, and re-layouts: 29.4 us -> 7.79 us
    ppermute x32 -> x16, waiting for transfers between devices: 42.4 us -> 63.5 us  [halving_scatter(): parts = keep + lax.ppermute(send, axis, route)]
    concatenate x0 -> x4, local copies, waits for them, and re-layouts: none -> 7.44 us  [the longest x2 4.43 us: shards(): jnp.concatenate([term.reshape(devices, -1) for term in node_terms], axis=1)]
    concatenate x0 -> x2, other arithmetic: none -> 4.95 us  [the longest x1 2.68 us: shards(): jnp.concatenate([term.reshape(devices, -1) for term in node_terms], axis=1)]
    add_any x0 -> x2, other arithmetic: none -> 3.24 us  [the longest x1 2.1 us: node_part(): w_node_in[:latent]]
    unnamed x105 -> x93, local copies, waits for them, and re-layouts: 16 us -> 12.9 us
    add x32 -> x16, other arithmetic: 12.1 us -> 9.63 us  [halving_scatter(): parts = keep + lax.ppermute(send, axis, route)]
  transfers between devices with their start and end apart: 44 -> 28, of which waited for: 13 -> 10; matrix products, arithmetic and copies ran while one was open for 28% -> 24% of each run, Pallas kernels for 0% -> 0%
where the time goes in v2:
time: 271 us; the launch traced here: 266 us
  local copies, waits for them, and re-layouts  73.5 us (27%)
  starting transfers between devices  67.5 us (25%)
  waiting for transfers between devices  63.5 us (23%)
  matrix products  33.2 us (12%)
  other arithmetic  26.4 us (10%)
    ppermute x16, waiting for transfers between devices, halving_scatter(): parts = keep + lax.ppermute(send, axis, route)  63.5 us
    ppermute x12, starting transfers between devices, passed_along(): return lax.ppermute(block, axis, route)  34 us
    ppermute x16, starting transfers between devices, halving_scatter(): parts = keep + lax.ppermute(send, axis, route)  33.5 us
    another operation x13, local copies, waits for them, and re-layouts, swap_faces(): jnp.stack([across_rows(face_blocks[1], 1), across_rows(face_blocks[0], -1...  20.1 us
    unnamed x93, local copies, waits for them, and re-layouts  12.9 us
    concatenate x1, local copies, waits for them, and re-layouts, edge_part(): extended = jnp.concatenate([node_blocks, received], axis=0)  10.9 us
    add x16, other arithmetic, halving_scatter(): parts = keep + lax.ppermute(send, axis, route)  9.63 us
    another operation x2, local copies, waits for them, and re-layouts  7.79 us
  transfers between devices with their start and end apart: 28, of which 10 were waited for; matrix products, arithmetic and copies ran while one was open for 24% of the time, Pallas kernels for 0%

profile of v2, /device:TPU:16, one launch (start us, length us, event | category | flops | bytes accessed | tf_op | source)
XLA Modules:
  0.0 266.1 jit_solution(6343422626544211086)
XLA Ops:
  0.6 1.7 convolution_convert_fusion.4
  3.6 3.2 %collective-permute-start = (bf16[128,512]{1,0:T(8,128)(2,1)S(1)}, bf16[128,512]{1,0:T(8,128)(2,1)S(1)}, u32[]{:S(2)}, u32[]{:S(2)}) collective-permute-start(bf16[128,512]{1,0:T(8,128)(2,1)S(1)} %bitcast.233), channel_id=1, source_target_pairs={{0,16},{16,32},{32,48},{48,64},{64,80},{80,96},{96,112},{1,17},{17... | collective-permute-start | bytes 393224 | tf_op jit(solution)/shard_map/ppermute | solution.py:12
  6.8 4.2 %collective-permute-start.1 = (bf16[128,512]{1,0:T(8,128)(2,1)S(1)}, bf16[128,512]{1,0:T(8,128)(2,1)S(1)}, u32[]{:S(2)}, u32[]{:S(2)}) collective-permute-start(bf16[128,512]{1,0:T(8,128)(2,1)S(1)} %bitcast.224), channel_id=1, source_target_pairs={{16,0},{32,16},{48,32},{64,48},{80,64},{96,80},{112,96},{17,1},{33... | collective-permute-start | bytes 393224 | tf_op jit(solution)/shard_map/ppermute | solution.py:12
  11.6 1.9 collective-permute-start.2
  16.3 3.8 %collective-permute-start.4 = (bf16[128,512]{1,0:T(8,128)(2,1)}, bf16[128,512]{1,0:T(8,128)(2,1)}, u32[]{:S(2)}, u32[]{:S(2)}) collective-permute-start(bf16[128,512]{1,0:T(8,128)(2,1)} %bitcast.196), channel_id=1, source_target_pairs={{0,128},{1,129},{2,130},{3,131},{4,132},{5,133},{6,134},{7,135},{8... | collective-permute-start | bytes 393224 | tf_op jit(solution)/shard_map/ppermute | solution.py:12
  20.2 2.0 fusion.32
  24.3 1.6 collective-permute-start.5
  32.1 1.8 copy.192
  34.0 1.8 copy.193
  35.8 1.8 copy.194
  37.6 1.8 copy.195
  39.4 10.9 %concatenate.25 = bf16[10,128,512]{2,0,1:T(8,128)(2,1)} concatenate(bf16[4,128,512]{2,0,1:T(4,128)(2,1)} %copy.189, bf16[1,128,512]{2,0,1:T(2,128)(2,1)} %copy.190, bf16[1,128,512]{2,0,1:T(2,128)(2,1)} %copy.191, bf16[1,128,512]{2,0,1:T(2,128)(2,1)} %copy.192, bf16[1,128,512]{2,0,1:T(2,128)(2,1)} %copy.193, bf16[1,128,512]{2,0,1:T(2,128)(2,1)} %copy.194, bf16[1,128,512]{2,0,1:T(2,128)(2,1)} %copy.195), dimensions={0} | concatenate | bytes 2621440 | tf_op jit(solution)/shard_map/jvp()/concatenate | solution.py:43
  50.3 2.2 convolution_convert_fusion.5
  61.7 1.6 convolution_convert_fusion.8
  67.3 1.8 fusion.60
  69.1 1.8 fusion.13
  72.1 1.6 fusion.65
  73.7 1.6 fusion.19
  75.3 1.7 convolution_convert_fusion.1
  77.0 2.2 concatenate.31
  79.2 2.1 pad_add_fusion.1
  81.3 2.3 concatenate.30
  86.1 2.4 fusion.17
  89.1 1.7 copy.201
  91.9 1.6 concatenate.26
  93.5 2.7 %maximum_convert_fusion.1 = f32[2,2,2,2,2,2,2,2,3072]{8,7,6,5,4,3,2,1,0:T(2,128)S(1)} fusion(bf16[2,2,2,2,2,2,2,2,1024]{8,7,6,5,4,3,2,1,0:T(2,128)(2,1)} %concatenate.31, bf16[2,2,2,2,2,2,2,2,2048]{8,7,6,5,4,3,2,1,0:T(2,128)(2,1)S(1)} %copy-done.15), kind=kLoop, calls=%fused_computation.26 | loop fusion | flops 3145728 | bytes 4718592 | tf_op jit(solution)/shard_map/concatenate | solution.py:172
  96.2 3.3 %constant_dynamic-slice_fusion.8 = (f32[2,2,2,2,2,2,2,1,3072]{8,7,6,5,4,3,2,1,0:T(1,128)S(1)}, f32[1,2,2,2,2,2,2,2,3072]{8,0,1,5,6,4,2,7,3:T(1,128)S(1)}) fusion(f32[2,2,2,2,2,2,2,2,3072]{8,7,6,5,4,3,2,1,0:T(2,128)S(1)} %maximum_convert_fusion.1, s32[]{:T(128)S(6)} %select_n.80, s32[]{:T(128)S(6)} %select_n.81), kind=kLoop, calls=%fused_computation.135 | loop fusion | bytes 6291464 | tf_op jit(solution)/shard_map/dynamic-slice.2
  99.6 2.0 copy.286
  101.6 2.5 collective-permute-start.20
  104.1 2.3 maximum_convert_fusion
  106.4 4.5 %constant_dynamic-slice_fusion.15 = (f32[2,2,2,2,2,2,2,1,4096]{8,7,6,5,4,3,2,1,0:T(1,128)S(1)}, f32[1,2,2,2,2,2,2,2,4096]{8,0,2,4,7,5,3,6,1:T(1,128)S(1)}) fusion(f32[2,2,2,2,2,2,2,2,4096]{8,7,6,5,4,3,2,1,0:T(2,128)S(1)} %maximum_convert_fusion, s32[]{:T(128)S(6)} %select_n.80, s32[]{:T(128)S(6)} %select_n.81), kind=kLoop, calls=%fused_computation.142 | loop fusion | bytes 8388616 | tf_op jit(solution)/shard_map/dynamic-slice
  110.9 1.9 copy.285
  116.4 4.4 %collective-permute-start.6 = (bf16[128,512]{1,0:T(8,128)(2,1)S(1)}, bf16[128,512]{1,0:T(8,128)(2,1)S(1)}, u32[]{:S(2)}, u32[]{:S(2)}) collective-permute-start(bf16[128,512]{1,0:T(8,128)(2,1)S(1)} %bitcast.232), channel_id=1, source_target_pairs={{0,16},{16,32},{32,48},{48,64},{64,80},{80,96},{96,112},{1,17},{17... | collective-permute-start | bytes 393224 | tf_op jit(solution)/shard_map/ppermute | solution.py:12
  120.8 3.0 %collective-permute-start.7 = (bf16[128,512]{1,0:T(8,128)(2,1)S(1)}, bf16[128,512]{1,0:T(8,128)(2,1)S(1)}, u32[]{:S(2)}, u32[]{:S(2)}) collective-permute-start(bf16[128,512]{1,0:T(8,128)(2,1)S(1)} %bitcast.231), channel_id=1, source_target_pairs={{16,0},{32,16},{48,32},{64,48},{80,64},{96,80},{112,96},{17,1},{33... | collective-permute-start | bytes 393224 | tf_op jit(solution)/shard_map/ppermute | solution.py:12
  123.8 1.8 collective-permute-start.8
  126.2 1.5 collective-permute-start.9
  127.7 2.5 fusion.8
  130.2 1.7 constant_dynamic-slice_fusion.7
  132.3 4.9 %collective-permute-start.21 = (f32[2,2,2,2,2,2,3072]{6,3,4,2,0,5,1:T(2,128)S(1)}, f32[2,2,2,2,2,2,3072]{6,3,4,2,0,5,1:T(2,128)S(1)}, u32[]{:S(2)}, u32[]{:S(2)}) collective-permute-start(f32[2,2,2,2,2,2,3072]{6,3,4,2,0,5,1:T(2,128)S(1)} %bitcast.219), channel_id=1, source_target_pairs={{0,2},{1,3},{2,0},{3,1},{4,6},{5,7},{6,4},{7,5},{8,10},{9,11},{10,... | collective-permute-start | bytes 2359304 | tf_op jit(solution)/shard_map/ppermute | solution.py:28
  137.2 2.2 fusion.2
  139.5 15.8 %collective-permute-done.21 = f32[2,2,2,2,2,2,3072]{6,3,4,2,0,5,1:T(2,128)S(1)} collective-permute-done((f32[2,2,2,2,2,2,3072]{6,3,4,2,0,5,1:T(2,128)S(1)}, f32[2,2,2,2,2,2,3072]{6,3,4,2,0,5,1:T(2,128)S(1)}, u32[]{:S(2)}, u32[]{:S(2)}) %collective-permute-start.21) | collective-permute-done | bytes 786464 | tf_op jit(solution)/shard_map/ppermute | solution.py:28
  155.8 1.6 collective-permute-start.22
  158.4 8.2 %collective-permute-done.22 = f32[2,2,2,2,2,3072]{5,2,3,1,4,0:T(2,128)S(1)} collective-permute-done((f32[2,2,2,2,2,3072]{5,2,3,1,4,0:T(2,128)S(1)}, f32[2,2,2,2,2,3072]{5,2,3,1,4,0:T(2,128)S(1)}, u32[]{:S(2)}, u32[]{:S(2)}) %collective-permute-start.22) | collective-permute-done | bytes 393248 | tf_op jit(solution)/shard_map/ppermute | solution.py:28
  166.7 5.8 %collective-permute-start.10 = (bf16[128,512]{1,0:T(8,128)(2,1)}, bf16[128,512]{1,0:T(8,128)(2,1)}, u32[]{:S(2)}, u32[]{:S(2)}) collective-permute-start(bf16[128,512]{1,0:T(8,128)(2,1)} %bitcast.190), channel_id=1, source_target_pairs={{0,128},{1,129},{2,130},{3,131},{4,132},{5,133},{6,134},{7,135},{8... | collective-permute-start | bytes 393224 | tf_op jit(solution)/shard_map/ppermute | solution.py:12
  174.7 3.3 %collective-permute-start.13 = (f32[2,2,2,2,2,2,4096]{6,0,2,5,3,1,4:T(2,128)}, f32[2,2,2,2,2,2,4096]{6,0,2,5,3,1,4:T(2,128)}, u32[]{:S(2)}, u32[]{:S(2)}) collective-permute-start(f32[2,2,2,2,2,2,4096]{6,0,2,5,3,1,4:T(2,128)} %dynamic-slice_bitcast_fusion.2), channel_id=1, source_target_pairs={{0,128},{128,0},{1,129},{129,1},{2,130},{130,2},{3,131},{131,3},{4... | collective-permute-start | bytes 3145736 | tf_op jit(solution)/shard_map/ppermute | solution.py:28
  178.1 2.3 convolution_convert_fusion.12
  184.3 1.8 copy.208
  186.1 1.8 copy.209
  187.9 5.7 %stack.51 = bf16[6,128,512]{2,0,1:T(8,128)(2,1)} concatenate(bf16[1,128,512]{2,0,1:T(2,128)(2,1)S(1)} %copy.204, bf16[1,128,512]{2,0,1:T(2,128)(2,1)S(1)} %copy.205, bf16[1,128,512]{2,0,1:T(2,128)(2,1)S(1)} %copy.206, bf16[1,128,512]{2,0,1:T(2,128)(2,1)S(1)} %copy.207, bf16[1,128,512]{2,0,1:T(2,128)(2,1)} %copy.208, bf16[1,128,512]{2,0,1:T(2,128)(2,1)} %copy.209), dimensions={0} | concatenate | bytes 1572864 | tf_op jit(solution)/shard_map/stack | solution.py:101
  193.6 12.7 %collective-permute-done.23 = f32[2,2,2,2,3072]{4,1,2,0,3:T(2,128)} collective-permute-done((f32[2,2,2,2,3072]{4,1,2,0,3:T(2,128)}, f32[2,2,2,2,3072]{4,1,2,0,3:T(2,128)}, u32[]{:S(2)}, u32[]{:S(2)}) %collective-permute-start.23) | collective-permute-done | bytes 196640 | tf_op jit(solution)/shard_map/ppermute | solution.py:28
  207.3 2.9 %collective-permute-start.24 = (f32[2,2,2,3072]{3,0,1,2:T(2,128)S(1)}, f32[2,2,2,3072]{3,0,1,2:T(2,128)S(1)}, u32[]{:S(2)}, u32[]{:S(2)}) collective-permute-start(f32[2,2,2,3072]{3,0,1,2:T(2,128)S(1)} %dynamic-slice_bitcast_fusion.6), channel_id=1, source_target_pairs={{0,16},{16,0},{32,48},{48,32},{64,80},{80,64},{96,112},{112,96},{1... | collective-permute-start | bytes 294920 | tf_op jit(solution)/shard_map/ppermute | solution.py:28
  210.2 2.1 bitcast_add_fusion.1
  213.9 1.5 collective-permute-start.14
  215.6 5.0 %collective-permute-start.25 = (f32[2,2,3072]{2,0,1:T(2,128)S(1)}, f32[2,2,3072]{2,0,1:T(2,128)S(1)}, u32[]{:S(2)}, u32[]{:S(2)}) collective-permute-start(f32[2,2,3072]{2,0,1:T(2,128)S(1)} %bitcast.236), channel_id=1, source_target_pairs={{0,4},{1,5},{2,6},{3,7},{4,0},{5,1},{6,2},{7,3},{8,12},{9,13},{10,... | collective-permute-start | bytes 147464 | tf_op jit(solution)/shard_map/ppermute | solution.py:28
  220.6 5.9 %collective-permute-done.14 = f32[2,2,2,2,2,4096]{5,1,4,2,0,3:T(2,128)S(1)} collective-permute-done((f32[2,2,2,2,2,4096]{5,1,4,2,0,3:T(2,128)S(1)}, f32[2,2,2,2,2,4096]{5,1,4,2,0,3:T(2,128)S(1)}, u32[]{:S(2)}, u32[]{:S(2)}) %collective-permute-start.14) | collective-permute-done | bytes 524320 | tf_op jit(solution)/shard_map/ppermute | solution.py:28
  228.5 5.1 %collective-permute-done.15 = f32[2,2,2,2,4096]{4,0,3,1,2:T(2,128)S(1)} collective-permute-done((f32[2,2,2,2,4096]{4,0,3,1,2:T(2,128)S(1)}, f32[2,2,2,2,4096]{4,0,3,1,2:T(2,128)S(1)}, u32[]{:S(2)}, u32[]{:S(2)}) %collective-permute-start.15) | collective-permute-done | bytes 262176 | tf_op jit(solution)/shard_map/ppermute | solution.py:28
  234.2 5.6 %collective-permute-start.16 = (f32[2,2,2,4096]{3,2,0,1:T(2,128)S(1)}, f32[2,2,2,4096]{3,2,0,1:T(2,128)S(1)}, u32[]{:S(2)}, u32[]{:S(2)}) collective-permute-start(f32[2,2,2,4096]{3,2,0,1:T(2,128)S(1)} %bitcast.234), channel_id=1, source_target_pairs={{0,4},{1,5},{2,6},{3,7},{4,0},{5,1},{6,2},{7,3},{8,12},{9,13},{10,... | collective-permute-start | bytes 393224 | tf_op jit(solution)/shard_map/ppermute | solution.py:28
  239.9 5.1 %collective-permute-done.16 = f32[2,2,2,4096]{3,2,0,1:T(2,128)S(1)} collective-permute-done((f32[2,2,2,4096]{3,2,0,1:T(2,128)S(1)}, f32[2,2,2,4096]{3,2,0,1:T(2,128)S(1)}, u32[]{:S(2)}, u32[]{:S(2)}) %collective-permute-start.16) | collective-permute-done | bytes 131104 | tf_op jit(solution)/shard_map/ppermute | solution.py:28
  245.3 2.3 collective-permute-done.26
  247.7 3.4 %collective-permute-done.17 = f32[2,2,4096]{2,1,0:T(2,128)S(1)} collective-permute-done((f32[2,2,4096]{2,1,0:T(2,128)S(1)}, f32[2,2,4096]{2,1,0:T(2,128)S(1)}, u32[]{:S(2)}, u32[]{:S(2)}) %collective-permute-start.17) | collective-permute-done | bytes 65568 | tf_op jit(solution)/shard_map/ppermute | solution.py:28
  251.1 1.4 collective-permute-start.18
  252.6 2.3 collective-permute-start.27
  254.9 1.8 collective-permute-done.18
  261.3 3.1 %collective-permute-done.19 = f32[4096]{0:T(1024)S(1)} collective-permute-done((f32[4096]{0:T(1024)S(1)}, f32[4096]{0:T(1024)S(1)}, u32[]{:S(2)}, u32[]{:S(2)}) %collective-permute-start.19) | collective-permute-done | bytes 16416 | tf_op jit(solution)/shard_map/ppermute | solution.py:28
  (194 shorter events, 55.1 us)
Async XLA Ops:
  0.6 53.5 %copy-start = (bf16[512,512]{1,0:T(8,128)(2,1)S(1)}, bf16[512,512]{1,0:T(8,128)(2,1)}, u32[]{:S(2)}) copy-start(bf16[512,512]{1,0:T(8,128)(2,1)} %param.19) | copy-start | bytes 1572868
  2.3 17.8 %copy-start.3 = (bf16[1024,512]{1,0:T(8,128)(2,1)S(1)}, bf16[1024,512]{1,0:T(8,128)(2,1)}, u32[]{:S(2)}) copy-start(bf16[1024,512]{1,0:T(8,128)(2,1)} %param.13) | copy-start | bytes 3145732
  2.3 17.8 %copy-start.16 = (bf16[1536,512]{1,0:T(8,128)(2,1)S(1)}, bf16[1536,512]{1,0:T(8,128)(2,1)}, u32[]{:S(2)}) copy-start(bf16[1536,512]{1,0:T(8,128)(2,1)} %param.18) | copy-start | bytes 4718596
  3.6 20.7 %collective-permute-start = (bf16[128,512]{1,0:T(8,128)(2,1)S(1)}, bf16[128,512]{1,0:T(8,128)(2,1)S(1)}, u32[]{:S(2)}, u32[]{:S(2)}) collective-permute-start(bf16[128,512]{1,0:T(8,128)(2,1)S(1)} %bitcast.233), channel_id=1, source_target_pairs={{0,16},{16,32},{32,48},{48,64},{64,80},{80,96},{96,112},{1,17},{17... | collective-permute-start | bytes 393224 | tf_op jit(solution)/shard_map/ppermute | solution.py:12
  6.8 24.5 %collective-permute-start.1 = (bf16[128,512]{1,0:T(8,128)(2,1)S(1)}, bf16[128,512]{1,0:T(8,128)(2,1)S(1)}, u32[]{:S(2)}, u32[]{:S(2)}) collective-permute-start(bf16[128,512]{1,0:T(8,128)(2,1)S(1)} %bitcast.224), channel_id=1, source_target_pairs={{16,0},{32,16},{48,32},{64,48},{80,64},{96,80},{112,96},{17,1},{33... | collective-permute-start | bytes 393224 | tf_op jit(solution)/shard_map/ppermute | solution.py:12
  11.6 20.5 %collective-permute-start.2 = (bf16[128,512]{1,0:T(8,128)(2,1)}, bf16[128,512]{1,0:T(8,128)(2,1)}, u32[]{:S(2)}, u32[]{:S(2)}) collective-permute-start(bf16[128,512]{1,0:T(8,128)(2,1)} %bitcast.198), channel_id=1, source_target_pairs={{0,1},{1,2},{2,3},{3,4},{4,5},{5,6},{6,7},{7,8},{8,9},{9,10},{10,1... | collective-permute-start | bytes 393224 | tf_op jit(solution)/shard_map/ppermute | solution.py:12
  14.2 8.0 %copy-start.2 = (bf16[512,512]{1,0:T(8,128)(2,1)S(1)}, bf16[512,512]{1,0:T(8,128)(2,1)}, u32[]{:S(2)}) copy-start(bf16[512,512]{1,0:T(8,128)(2,1)} %param.12) | copy-start | bytes 1572868
  14.2 19.7 %collective-permute-start.3 = (bf16[128,512]{1,0:T(8,128)(2,1)}, bf16[128,512]{1,0:T(8,128)(2,1)}, u32[]{:S(2)}, u32[]{:S(2)}) collective-permute-start(bf16[128,512]{1,0:T(8,128)(2,1)} %bitcast.197), channel_id=1, source_target_pairs={{1,0},{2,1},{3,2},{4,3},{5,4},{6,5},{7,6},{8,7},{9,8},{10,9},{11,1... | collective-permute-start | bytes 393224 | tf_op jit(solution)/shard_map/ppermute | solution.py:12
  16.3 19.5 %collective-permute-start.4 = (bf16[128,512]{1,0:T(8,128)(2,1)}, bf16[128,512]{1,0:T(8,128)(2,1)}, u32[]{:S(2)}, u32[]{:S(2)}) collective-permute-start(bf16[128,512]{1,0:T(8,128)(2,1)} %bitcast.196), channel_id=1, source_target_pairs={{0,128},{1,129},{2,130},{3,131},{4,132},{5,133},{6,134},{7,135},{8... | collective-permute-start | bytes 393224 | tf_op jit(solution)/shard_map/ppermute | solution.py:12
  22.2 3.7 %copy-start.18 = (bf16[1024,512]{1,0:T(8,128)(2,1)S(1)}, bf16[1024,512]{1,0:T(8,128)(2,1)}, u32[]{:S(2)}) copy-start(bf16[1024,512]{1,0:T(8,128)(2,1)} %param.20) | copy-start | bytes 3145732
  24.3 4.5 %copy-start.33 = (s32[4,2]{0,1:T(2,128)S(1)}, s32[4,2]{0,1:T(2,128)}, u32[]{:S(2)}) copy-start(s32[4,2]{0,1:T(2,128)} %param.16) | copy-start | bytes 100
  24.3 4.6 %copy-start.32 = (s32[4,2]{0,1:T(2,128)S(1)}, s32[4,2]{0,1:T(2,128)}, u32[]{:S(2)}) copy-start(s32[4,2]{0,1:T(2,128)} %param.15) | copy-start | bytes 100
  24.3 13.3 %collective-permute-start.5 = (bf16[128,512]{1,0:T(8,128)(2,1)}, bf16[128,512]{1,0:T(8,128)(2,1)}, u32[]{:S(2)}, u32[]{:S(2)}) collective-permute-start(bf16[128,512]{1,0:T(8,128)(2,1)} %bitcast.195), channel_id=1, source_target_pairs={{128,0},{129,1},{130,2},{131,3},{132,4},{133,5},{134,6},{135,7},{1... | collective-permute-start | bytes 393224 | tf_op jit(solution)/shard_map/ppermute | solution.py:12
  39.4 13.2 %copy-start.28 = (bf16[4,2,128,128]{3,2,1,0:T(8,128)(2,1)S(1)}, bf16[4,2,128,128]{3,2,1,0:T(8,128)(2,1)}, u32[]{:S(2)}) copy-start(bf16[4,2,128,128]{3,2,1,0:T(8,128)(2,1)} %param.14) | copy-start | bytes 786436
  50.3 3.1 %copy-start.6 = (f32[1024,512]{1,0:T(8,128)S(1)}, f32[1024,512]{1,0:T(8,128)}, u32[]{:S(2)}) copy-start(f32[1024,512]{1,0:T(8,128)} %fusion.32) | copy-start | bytes 6291460
  50.3 3.1 %copy-start.14 = (f32[512,512]{1,0:T(8,128)S(1)}, f32[512,512]{1,0:T(8,128)}, u32[]{:S(2)}) copy-start(f32[512,512]{1,0:T(8,128)} %fusion.37) | copy-start | bytes 3145732
  50.3 3.1 %copy-start.17 = (bf16[1536,512]{1,0:T(8,128)(2,1)S(1)}, bf16[1536,512]{1,0:T(8,128)(2,1)}, u32[]{:S(2)}) copy-start(bf16[1536,512]{1,0:T(8,128)(2,1)} %param.18) | copy-start | bytes 4718596
  56.9 1.2 copy-start.8
  56.9 1.5 copy-start.19
  57.2 1.7 copy-start.34
  61.7 4.2 %copy-start.23 = (bf16[512,512]{1,0:T(8,128)(2,1)}, bf16[512,512]{1,0:T(8,128)(2,1)S(1)}, u32[]{:S(2)}) copy-start(bf16[512,512]{1,0:T(8,128)(2,1)S(1)} %fusion.23) | copy-start | bytes 1572868
  64.5 1.9 copy-start.12
  72.1 1.6 copy-start.4
  75.3 3.9 %copy-start.25 = (bf16[512,512]{1,0:T(8,128)(2,1)S(1)}, bf16[512,512]{1,0:T(8,128)(2,1)}, u32[]{:S(2)}) copy-start(bf16[512,512]{1,0:T(8,128)(2,1)} %fusion.18) | copy-start | bytes 1572868
  86.1 2.5 copy-start.11
  88.5 2.2 copy-start.26
  88.5 2.2 copy-start.27
  91.9 1.6 copy-start.15
  99.6 4.5 %copy-start.7 = (bf16[2,2,2,2,2,2,2,2,3072]{8,7,6,5,4,3,2,1,0:T(2,128)(2,1)S(1)}, bf16[2,2,2,2,2,2,2,2,3072]{8,7,6,5,4,3,2,1,0:T(2,128)(2,1)}, u32[]{:S(2)}) copy-start(bf16[2,2,2,2,2,2,2,2,3072]{8,7,6,5,4,3,2,1,0:T(2,128)(2,1)} %concatenate.26) | copy-start | bytes 4718596
  101.6 24.6 %collective-permute-start.20 = (f32[2,2,2,2,2,2,2,3072]{7,0,4,5,3,1,6,2:T(2,128)}, f32[2,2,2,2,2,2,2,3072]{7,0,4,5,3,1,6,2:T(2,128)}, u32[]{:S(2)}, u32[]{:S(2)}) collective-permute-start(f32[2,2,2,2,2,2,2,3072]{7,0,4,5,3,1,6,2:T(2,128)} %bitcast.185), channel_id=1, source_target_pairs={{0,1},{1,0},{2,3},{3,2},{4,5},{5,4},{6,7},{7,6},{8,9},{9,8},{10,11... | collective-permute-start | bytes 4718600 | tf_op jit(solution)/shard_map/ppermute | solution.py:28
  110.8 2.1 copy-start.13
  112.8 19.5 %collective-permute-start.12 = (f32[2,2,2,2,2,2,2,4096]{7,1,3,6,4,2,5,0:T(2,128)S(1)}, f32[2,2,2,2,2,2,2,4096]{7,1,3,6,4,2,5,0:T(2,128)S(1)}, u32[]{:S(2)}, u32[]{:S(2)}) collective-permute-start(f32[2,2,2,2,2,2,2,4096]{7,1,3,6,4,2,5,0:T(2,128)S(1)} %bitcast.211), channel_id=1, source_target_pairs={{0,1},{1,0},{2,3},{3,2},{4,5},{5,4},{6,7},{7,6},{8,9},{9,8},{10,11... | collective-permute-start | bytes 6291464 | tf_op jit(solution)/shard_map/ppermute | solution.py:28
  113.7 11.9 %copy-start.20 = (bf16[1024,512]{1,0:T(8,128)(2,1)S(1)}, bf16[1024,512]{1,0:T(8,128)(2,1)}, u32[]{:S(2)}) copy-start(bf16[1024,512]{1,0:T(8,128)(2,1)} %param.20) | copy-start | bytes 3145732
  113.7 11.9 %copy-start.24 = (bf16[512,512]{1,0:T(8,128)(2,1)S(1)}, bf16[512,512]{1,0:T(8,128)(2,1)}, u32[]{:S(2)}) copy-start(bf16[512,512]{1,0:T(8,128)(2,1)} %copy-done.23) | copy-start | bytes 1572868
  113.7 11.9 %copy-start.30 = (bf16[512,512]{1,0:T(8,128)(2,1)S(1)}, bf16[512,512]{1,0:T(8,128)(2,1)}, u32[]{:S(2)}) copy-start(bf16[512,512]{1,0:T(8,128)(2,1)} %param.22) | copy-start | bytes 1572868
  116.4 57.0 %collective-permute-start.6 = (bf16[128,512]{1,0:T(8,128)(2,1)S(1)}, bf16[128,512]{1,0:T(8,128)(2,1)S(1)}, u32[]{:S(2)}, u32[]{:S(2)}) collective-permute-start(bf16[128,512]{1,0:T(8,128)(2,1)S(1)} %bitcast.232), channel_id=1, source_target_pairs={{0,16},{16,32},{32,48},{48,64},{64,80},{80,96},{96,112},{1,17},{17... | collective-permute-start | bytes 393224 | tf_op jit(solution)/shard_map/ppermute | solution.py:12
  120.8 53.9 %collective-permute-start.7 = (bf16[128,512]{1,0:T(8,128)(2,1)S(1)}, bf16[128,512]{1,0:T(8,128)(2,1)S(1)}, u32[]{:S(2)}, u32[]{:S(2)}) collective-permute-start(bf16[128,512]{1,0:T(8,128)(2,1)S(1)} %bitcast.231), channel_id=1, source_target_pairs={{16,0},{32,16},{48,32},{64,48},{80,64},{96,80},{112,96},{17,1},{33... | collective-permute-start | bytes 393224 | tf_op jit(solution)/shard_map/ppermute | solution.py:12
  123.8 54.2 %collective-permute-start.8 = (bf16[128,512]{1,0:T(8,128)(2,1)S(1)}, bf16[128,512]{1,0:T(8,128)(2,1)S(1)}, u32[]{:S(2)}, u32[]{:S(2)}) collective-permute-start(bf16[128,512]{1,0:T(8,128)(2,1)S(1)} %bitcast.230), channel_id=1, source_target_pairs={{0,1},{1,2},{2,3},{3,4},{4,5},{5,6},{6,7},{7,8},{8,9},{9,10},{10,1... | collective-permute-start | bytes 393224 | tf_op jit(solution)/shard_map/ppermute | solution.py:12
  126.2 57.0 %collective-permute-start.9 = (bf16[128,512]{1,0:T(8,128)(2,1)S(1)}, bf16[128,512]{1,0:T(8,128)(2,1)}, u32[]{:S(2)}, u32[]{:S(2)}) collective-permute-start(bf16[128,512]{1,0:T(8,128)(2,1)S(1)} %bitcast.226), channel_id=1, source_target_pairs={{1,0},{2,1},{3,2},{4,3},{5,4},{6,5},{7,6},{8,7},{9,8},{10,9},{11,1... | collective-permute-start | bytes 393224 | tf_op jit(solution)/shard_map/ppermute | solution.py:12
  132.3 22.9 %collective-permute-start.21 = (f32[2,2,2,2,2,2,3072]{6,3,4,2,0,5,1:T(2,128)S(1)}, f32[2,2,2,2,2,2,3072]{6,3,4,2,0,5,1:T(2,128)S(1)}, u32[]{:S(2)}, u32[]{:S(2)}) collective-permute-start(f32[2,2,2,2,2,2,3072]{6,3,4,2,0,5,1:T(2,128)S(1)} %bitcast.219), channel_id=1, source_target_pairs={{0,2},{1,3},{2,0},{3,1},{4,6},{5,7},{6,4},{7,5},{8,10},{9,11},{10,... | collective-permute-start | bytes 2359304 | tf_op jit(solution)/shard_map/ppermute | solution.py:28
  139.4 19.0 %copy-start.5 = (f32[2,2,2,2,2,2,2,4096]{7,1,3,6,4,2,5,0:T(2,128)}, f32[2,2,2,2,2,2,2,4096]{7,1,3,6,4,2,5,0:T(2,128)S(1)}, u32[]{:S(2)}) copy-start(f32[2,2,2,2,2,2,2,4096]{7,1,3,6,4,2,5,0:T(2,128)S(1)} %fusion.2) | copy-start | bytes 6291460
  155.8 22.3 %copy-start.22 = (bf16[4,128,512]{2,1,0:T(8,128)(2,1)S(1)}, bf16[4,128,512]{2,1,0:T(8,128)(2,1)}, u32[]{:S(2)}) copy-start(bf16[4,128,512]{2,1,0:T(8,128)(2,1)} %reduce_sum.115) | copy-start | bytes 1572868
  155.8 10.8 %collective-permute-start.22 = (f32[2,2,2,2,2,3072]{5,2,3,1,4,0:T(2,128)S(1)}, f32[2,2,2,2,2,3072]{5,2,3,1,4,0:T(2,128)S(1)}, u32[]{:S(2)}, u32[]{:S(2)}) collective-permute-start(f32[2,2,2,2,2,3072]{5,2,3,1,4,0:T(2,128)S(1)} %dynamic-slice_bitcast_fusion.3), channel_id=1, source_target_pairs={{0,32},{16,48},{32,0},{48,16},{64,96},{80,112},{96,64},{112,80},{1... | collective-permute-start | bytes 1179656 | tf_op jit(solution)/shard_map/ppermute | solution.py:28
  166.7 17.7 %collective-permute-start.10 = (bf16[128,512]{1,0:T(8,128)(2,1)}, bf16[128,512]{1,0:T(8,128)(2,1)}, u32[]{:S(2)}, u32[]{:S(2)}) collective-permute-start(bf16[128,512]{1,0:T(8,128)(2,1)} %bitcast.190), channel_id=1, source_target_pairs={{0,128},{1,129},{2,130},{3,131},{4,132},{5,133},{6,134},{7,135},{8... | collective-permute-start | bytes 393224 | tf_op jit(solution)/shard_map/ppermute | solution.py:12
  172.7 8.8 %copy-start.21 = (bf16[512,512]{0,1:T(8,128)(2,1)S(1)}, bf16[512,512]{0,1:T(8,128)(2,1)}, u32[]{:S(2)}) copy-start(bf16[512,512]{0,1:T(8,128)(2,1)} %get-tuple-element.82) | copy-start | bytes 1572868
  173.4 12.7 %collective-permute-start.11 = (bf16[128,512]{1,0:T(8,128)(2,1)}, bf16[128,512]{1,0:T(8,128)(2,1)}, u32[]{:S(2)}, u32[]{:S(2)}) collective-permute-start(bf16[128,512]{1,0:T(8,128)(2,1)} %bitcast.189), channel_id=1, source_target_pairs={{128,0},{129,1},{130,2},{131,3},{132,4},{133,5},{134,6},{135,7},{1... | collective-permute-start | bytes 393224 | tf_op jit(solution)/shard_map/ppermute | solution.py:12
  174.7 35.5 %collective-permute-start.13 = (f32[2,2,2,2,2,2,4096]{6,0,2,5,3,1,4:T(2,128)}, f32[2,2,2,2,2,2,4096]{6,0,2,5,3,1,4:T(2,128)}, u32[]{:S(2)}, u32[]{:S(2)}) collective-permute-start(f32[2,2,2,2,2,2,4096]{6,0,2,5,3,1,4:T(2,128)} %dynamic-slice_bitcast_fusion.2), channel_id=1, source_target_pairs={{0,128},{128,0},{1,129},{129,1},{2,130},{130,2},{3,131},{131,3},{4... | collective-permute-start | bytes 3145736 | tf_op jit(solution)/shard_map/ppermute | solution.py:28
  178.0 28.3 %collective-permute-start.23 = (f32[2,2,2,2,3072]{4,1,2,0,3:T(2,128)}, f32[2,2,2,2,3072]{4,1,2,0,3:T(2,128)}, u32[]{:S(2)}, u32[]{:S(2)}) collective-permute-start(f32[2,2,2,2,3072]{4,1,2,0,3:T(2,128)} %dynamic-slice_bitcast_fusion.5), channel_id=1, source_target_pairs={{0,128},{128,0},{1,129},{129,1},{2,130},{130,2},{3,131},{131,3},{4... | collective-permute-start | bytes 589832 | tf_op jit(solution)/shard_map/ppermute | solution.py:28
  207.3 8.1 %collective-permute-start.24 = (f32[2,2,2,3072]{3,0,1,2:T(2,128)S(1)}, f32[2,2,2,3072]{3,0,1,2:T(2,128)S(1)}, u32[]{:S(2)}, u32[]{:S(2)}) collective-permute-start(f32[2,2,2,3072]{3,0,1,2:T(2,128)S(1)} %dynamic-slice_bitcast_fusion.6), channel_id=1, source_target_pairs={{0,16},{16,0},{32,48},{48,32},{64,80},{80,64},{96,112},{112,96},{1... | collective-permute-start | bytes 294920 | tf_op jit(solution)/shard_map/ppermute | solution.py:28
  213.9 12.6 %collective-permute-start.14 = (f32[2,2,2,2,2,4096]{5,1,4,2,0,3:T(2,128)S(1)}, f32[2,2,2,2,2,4096]{5,1,4,2,0,3:T(2,128)S(1)}, u32[]{:S(2)}, u32[]{:S(2)}) collective-permute-start(f32[2,2,2,2,2,4096]{5,1,4,2,0,3:T(2,128)S(1)} %bitcast.222), channel_id=1, source_target_pairs={{0,2},{1,3},{2,0},{3,1},{4,6},{5,7},{6,4},{7,5},{8,10},{9,11},{10,... | collective-permute-start | bytes 1572872 | tf_op jit(solution)/shard_map/ppermute | solution.py:28
  215.6 12.8 %collective-permute-start.25 = (f32[2,2,3072]{2,0,1:T(2,128)S(1)}, f32[2,2,3072]{2,0,1:T(2,128)S(1)}, u32[]{:S(2)}, u32[]{:S(2)}) collective-permute-start(f32[2,2,3072]{2,0,1:T(2,128)S(1)} %bitcast.236), channel_id=1, source_target_pairs={{0,4},{1,5},{2,6},{3,7},{4,0},{5,1},{6,2},{7,3},{8,12},{9,13},{10,... | collective-permute-start | bytes 147464 | tf_op jit(solution)/shard_map/ppermute | solution.py:28
  227.1 30.5 %copy-start.9 = (f32[4,128,512]{2,1,0:T(8,128)S(1)}, f32[4,128,512]{2,1,0:T(8,128)}, u32[]{:S(2)}) copy-start(f32[4,128,512]{2,1,0:T(8,128)} %convert.8) | copy-start | bytes 3145732
  227.1 30.5 %copy-start.10 = (bf16[6,128,512]{2,0,1:T(8,128)(2,1)S(1)}, bf16[6,128,512]{2,0,1:T(8,128)(2,1)}, u32[]{:S(2)}) copy-start(bf16[6,128,512]{2,0,1:T(8,128)(2,1)} %stack.51) | copy-start | bytes 2359300
  227.1 30.5 %copy-start.29 = (bf16[512,512]{1,0:T(8,128)(2,1)S(1)}, bf16[512,512]{1,0:T(8,128)(2,1)}, u32[]{:S(2)}) copy-start(bf16[512,512]{1,0:T(8,128)(2,1)} %convolution_convert_fusion.12) | copy-start | bytes 1572868
  227.1 30.5 %copy-start.31 = (s32[1,6]{1,0:T(1,128)S(1)}, s32[1,6]{1,0:T(1,128)}, u32[]{:S(2)}) copy-start(s32[1,6]{1,0:T(1,128)} %param.17) | copy-start | bytes 76
  227.2 6.5 %collective-permute-start.15 = (f32[2,2,2,2,4096]{4,0,3,1,2:T(2,128)S(1)}, f32[2,2,2,2,4096]{4,0,3,1,2:T(2,128)S(1)}, u32[]{:S(2)}, u32[]{:S(2)}) collective-permute-start(f32[2,2,2,2,4096]{4,0,3,1,2:T(2,128)S(1)} %dynamic-slice_bitcast_fusion.4), channel_id=1, source_target_pairs={{0,32},{16,48},{32,0},{48,16},{64,96},{80,112},{96,64},{112,80},{1... | collective-permute-start | bytes 786440 | tf_op jit(solution)/shard_map/ppermute | solution.py:28
  234.2 10.9 %collective-permute-start.16 = (f32[2,2,2,4096]{3,2,0,1:T(2,128)S(1)}, f32[2,2,2,4096]{3,2,0,1:T(2,128)S(1)}, u32[]{:S(2)}, u32[]{:S(2)}) collective-permute-start(f32[2,2,2,4096]{3,2,0,1:T(2,128)S(1)} %bitcast.234), channel_id=1, source_target_pairs={{0,4},{1,5},{2,6},{3,7},{4,0},{5,1},{6,2},{7,3},{8,12},{9,13},{10,... | collective-permute-start | bytes 393224 | tf_op jit(solution)/shard_map/ppermute | solution.py:28
  239.8 7.8 %collective-permute-start.26 = (f32[2,3072]{1,0:T(2,128)S(1)}, f32[2,3072]{1,0:T(2,128)S(1)}, u32[]{:S(2)}, u32[]{:S(2)}) collective-permute-start(f32[2,3072]{1,0:T(2,128)S(1)} %bitcast.240), channel_id=1, source_target_pairs={{0,8},{1,9},{2,10},{3,11},{4,12},{5,13},{6,14},{7,15},{8,0},{9,1},... | collective-permute-start | bytes 73736 | tf_op jit(solution)/shard_map/ppermute | solution.py:28
  245.2 5.9 %collective-permute-start.17 = (f32[2,2,4096]{2,1,0:T(2,128)S(1)}, f32[2,2,4096]{2,1,0:T(2,128)S(1)}, u32[]{:S(2)}, u32[]{:S(2)}) collective-permute-start(f32[2,2,4096]{2,1,0:T(2,128)S(1)} %dynamic-slice_bitcast_fusion.7), channel_id=1, source_target_pairs={{0,16},{16,0},{32,48},{48,32},{64,80},{80,64},{96,112},{112,96},{1... | collective-permute-start | bytes 196616 | tf_op jit(solution)/shard_map/ppermute | solution.py:28
  251.1 5.5 %collective-permute-start.18 = (f32[2,4096]{1,0:T(2,128)S(1)}, f32[2,4096]{1,0:T(2,128)S(1)}, u32[]{:S(2)}, u32[]{:S(2)}) collective-permute-start(f32[2,4096]{1,0:T(2,128)S(1)} %dynamic-slice_bitcast_fusion.8), channel_id=1, source_target_pairs={{0,64},{16,80},{32,96},{48,112},{64,0},{80,16},{96,32},{112,48},{1... | collective-permute-start | bytes 98312 | tf_op jit(solution)/shard_map/ppermute | solution.py:28
  252.6 7.5 %collective-permute-start.27 = (f32[3072]{0:T(1024)S(1)}, f32[3072]{0:T(1024)S(1)}, u32[]{:S(2)}, u32[]{:S(2)}) collective-permute-start(f32[3072]{0:T(1024)S(1)} %bitcast.242), channel_id=1, source_target_pairs={{0,64},{16,80},{32,96},{48,112},{64,0},{80,16},{96,32},{112,48},{1... | collective-permute-start | bytes 36872 | tf_op jit(solution)/shard_map/ppermute | solution.py:28
  256.7 7.7 %collective-permute-start.19 = (f32[4096]{0:T(1024)S(1)}, f32[4096]{0:T(1024)S(1)}, u32[]{:S(2)}, u32[]{:S(2)}) collective-permute-start(f32[4096]{0:T(1024)S(1)} %bitcast.241), channel_id=1, source_target_pairs={{0,8},{1,9},{2,10},{3,11},{4,12},{5,13},{6,14},{7,15},{8,0},{9,1},... | collective-permute-start | bytes 49160 | tf_op jit(solution)/shard_map/ppermute | solution.py:28
  257.6 8.0 %copy-start.1 = (bf16[512,512]{1,0:T(8,128)(2,1)S(1)}, bf16[512,512]{1,0:T(8,128)(2,1)}, u32[]{:S(2)}) copy-start(bf16[512,512]{1,0:T(8,128)(2,1)} %param.19) | copy-start | bytes 1572868
